TPU v7x, 128 devices: a whole 4x4x4 slice. The times are simulated.
128 devices in a mesh: sta: 2 (over x_lo), gx: 16 (over x_hi, z, core), gy: 4 (over y).
Axes of the slice: x: 4 (x_hi: 2, x_lo: 2; x = x_hi * 2 + x_lo), y: 4, z: 4, core: 2. Of those that a mesh axis runs over, the one named last changes fastest.
Arguments:
- record: float32 [128, 1024], replicated, may hold values from -6 to 6
- shifts: int32 [128, 256], P(None, 'gx'), may hold values from 0 to 1022
- station_group: int32 [128], replicated, may hold values from 0 to 7
- weights: bfloat16 [128, 256, 512], P('sta', 'gy'), may hold values from -6 to 6
- psf_real: float32 [256, 256, 512], P(None, 'gx', 'gy'), may hold values from -6 to 6
- psf_imag: float32 [256, 256, 512], P(None, 'gx', 'gy'), may hold values from -6 to 6
Outputs:
- image: float32 [2, 256, 256, 512], P('sta', 'gx', 'gy')
All inputs are finite; a program needn't handle non-finite values.
Results may differ from a plain program's by a relative error of at most 0.0029.
Values may be sent and summed in bfloat16 or wider, within the bound.
No kernel may reach another device: no remote copies, remote signals or barrier semaphores. Data moves between devices by JAX's collectives and lax.ppermute only.
A program may use at most 128 MiB of HBM per device.

v0:
```python
import math

import jax
import jax.numpy as jnp
from jax import lax
from jax.sharding import PartitionSpec as P

T_DEV = 1
NZ = 256
NX = 256
GROUPS = 8


NOISE_POWER = 0.25
HIGHEST = lax.Precision.HIGHEST


def station_counts(station_group):
    labels = jnp.arange(GROUPS, dtype=jnp.int32)
    onehot = (station_group[:, None] == labels[None, :]).astype(jnp.float32)
    totals = jnp.sum(onehot, axis=0)
    return jnp.dot(onehot, totals, precision=HIGHEST)


def coefficients(record, shifts, per_station, first_time, num_times):
    times_range = first_time + jnp.arange(num_times, dtype=jnp.int32)
    positions = shifts[:, :, None] + times_range[None, None, :]
    values = jnp.take_along_axis(record, positions.reshape(positions.shape[0], -1), axis=1)
    scaled = values.reshape(positions.shape) / per_station[:, None, None]
    return jnp.transpose(scaled, (2, 1, 0)).astype(jnp.bfloat16)


def fourier_parts(length, scale):
    indices = jnp.arange(length, dtype=jnp.int32)
    product = indices[:, None] * indices[None, :] % length
    angles = product.astype(jnp.float32) * (2.0 * math.pi / length)
    return (jnp.cos(angles) * scale, jnp.sin(angles) * scale)


def complex_table(length, forward):
    if forward:
        cosine, sine = fourier_parts(length, 1.0)
        return jnp.stack([jnp.stack([cosine, sine]), jnp.stack([-sine, cosine])])
    cosine, sine = fourier_parts(length, 1.0 / length)
    return jnp.stack([jnp.stack([cosine, -sine]), jnp.stack([sine, cosine])])


def along_rows(piece, table):
    return jnp.einsum("itzny,oikn->otzky", piece, table, precision=HIGHEST)


def along_depth(piece, table):
    return jnp.einsum("itnxy,oikn->otkxy", piece, table, precision=HIGHEST)


def on_device(record, shifts, station_group, weights, psf_real, psf_imag):
    per_station = station_counts(station_group)
    depth_rows = shifts.shape[1]
    lateral_rows = weights.shape[1]
    width_y = weights.shape[2]
    columns = lateral_rows * width_y
    first_time = lax.axis_index("sta") * T_DEV
    coefficient = coefficients(record, shifts, per_station, first_time, T_DEV)
    coefficient = coefficient.reshape(T_DEV * depth_rows, coefficient.shape[2])
    piece = lax.all_gather(weights, "sta", axis=0, tiled=True)
    stack = jnp.dot(
        coefficient, piece.reshape(piece.shape[0], columns), preferred_element_type=jnp.float32
    )
    stack = stack.reshape(T_DEV, depth_rows, lateral_rows, width_y)
    cosine_y, sine_y = fourier_parts(width_y, 1.0)
    spectrum = jnp.einsum(
        "tzxn,okn->otzxk", stack, jnp.stack([cosine_y, -sine_y]), precision=HIGHEST
    )
    row_table = complex_table(NX, True)
    by_rows = along_rows(
        lax.all_to_all(spectrum, "gy", split_axis=4, concat_axis=3, tiled=True), row_table
    )
    depth_table = complex_table(NZ, True)
    by_depth = along_depth(
        lax.all_to_all(by_rows, "gx", split_axis=3, concat_axis=2, tiled=True), depth_table
    )
    power = psf_real * psf_real + psf_imag * psf_imag + NOISE_POWER
    filt_real = (psf_real * by_depth[0] + psf_imag * by_depth[1]) / power
    filt_imag = (psf_real * by_depth[1] - psf_imag * by_depth[0]) / power
    back_depth = along_depth(jnp.stack([filt_real, filt_imag]), complex_table(NZ, False))
    back_table = complex_table(NX, False)
    back_rows = along_rows(
        lax.all_to_all(back_depth, "gx", split_axis=2, concat_axis=3, tiled=True), back_table
    )
    cosine_back, sine_back = fourier_parts(width_y, 1.0 / width_y)
    real_table = jnp.stack([cosine_back, -sine_back])
    return jnp.einsum(
        "itzxk,iyk->tzxy",
        lax.all_to_all(back_rows, "gy", split_axis=3, concat_axis=4, tiled=True),
        real_table,
        precision=HIGHEST,
    )


def solution(mesh):
    in_specs = (
        P(),
        P(None, "gx"),
        P(),
        P("sta", "gy", None),
        P(None, "gx", "gy"),
        P(None, "gx", "gy"),
    )
    out_specs = P("sta", "gx", "gy", None)
    return jax.shard_map(
        on_device, mesh=mesh, in_specs=in_specs, out_specs=out_specs, check_vma=False
    )
```

profile of v0, /device:TPU:0, one launch (start us, length us, event | category | flops | bytes accessed | tf_op | source)
XLA Modules:
  0.0 516.7 jit_solution(10342550417236700609)
XLA Ops:
  7.6 16.6 %gather_fusion = f32[2048]{0:T(1024)S(1)} fusion(f32[128,1024]{1,0:T(8,128)S(1)} %copy-done, s32[2048]{0:T(1024)S(1)} %reshape.275), kind=kCustom, calls=%fused_computation | custom fusion | bytes 32768 | tf_op jit(solution)/shard_map/jit(take_along_axis)/gather | solution.py:28
  24.6 4.1 fusion.27
  28.7 89.3 %all-gather.2.cloned.1.call-done = bf16[128,64,512]{2,1,0:T(8,128)(2,1)} async-done(((bf16[64,64,512]{2,1,0:T(8,128)(2,1)}), bf16[128,64,512]{2,1,0:T(8,128)(2,1)}) %all-gather.2.cloned.1.call-update) | async-done | bytes 8388624 | tf_op jit(solution)/shard_map/all_gather | solution.py:65
  118.0 13.1 %copy.78 = bf16[128,64,512]{0,2,1:T(8,128)(2,1)} copy(bf16[128,64,512]{2,1,0:T(8,128)(2,1)} %all-gather.2.cloned.1.call-done) | data formatting | bytes 16777216 | tf_op jit(solution)/shard_map/reshape | solution.py:67
  131.1 5.8 %fusion = f32[16,64,512]{2,0,1:T(8,128)S(1)} fusion(bf16[128,64,512]{0,2,1:T(8,128)(2,1)} %copy.78, f32[128,16]{1,0:T(8,128)S(1)} %reshape.278, s32[128,16]{1,0:T(8,128)S(1)} %copy.50, f32[128]{0:T(128)S(1)} %convolution_bitcast_fusion.4, s32[]{:T(128)S(6)} %axis_index.15), kind=kOutput, calls=%fused_computation.1 | convolution fusion | flops 134238208 | bytes 10502660 | tf_op jit(solution)/shard_map/dot_general | solution.py:66
  136.9 9.2 %convolution_bitcast_fusion = f32[2,1,16,64,512]{4,3,2,0,1:T(8,128)} fusion(f32[1,512,512]{2,1,0:T(8,128)S(1)} %get-tuple-element.12, f32[1,512,512]{2,1,0:T(8,128)S(1)} %get-tuple-element.11, f32[16,64,512]{2,0,1:T(8,128)S(1)} %fusion), kind=kOutput, calls=%fused_computation.8 | convolution fusion | flops 6442975232 | bytes 8388608 | tf_op jit(solution)/shard_map/tzxn,okn->otzxk/dot_general | solution.py:71
  146.0 9.1 %copy.54 = f32[2,1,16,64,512]{3,2,0,1,4:T(8,128)} copy(f32[2,1,16,64,512]{4,3,2,0,1:T(8,128)} %convolution_bitcast_fusion) | data formatting | bytes 8388608 | tf_op jit(solution)/shard_map/tzxn,okn->otzxk/transpose | solution.py:71
  155.2 19.9 %reshape.303 = f32[4,1,262144]{2,1,0:T(1,128)} reshape(f32[512,1,2,16,64]{4,3,2,1,0:T(8,128)} %bitcast.153) | data formatting | bytes 8388608
  175.1 4.8 all-to-all-start
  182.1 47.0 %all-to-all-done = f32[4,1,262144]{2,1,0:T(1,128)} async-done(((f32[4,1,262144]{2,1,0:T(1,128)}), f32[4,1,262144]{2,1,0:T(1,128)}, u32[]{:S(2)}, u32[]{:S(2)}) %all-to-all-start) | async-done | bytes 4194336 | tf_op jit(solution)/shard_map/all_to_all | solution.py:76
  229.6 15.2 %reduce = f32[4,262144]{1,0:T(4,128)} reduce(f32[4,1,262144]{2,1,0:T(1,128)} %all-to-all-done, f32[]{:T(128)} %broadcast.479), dimensions={1}, to_apply=%all_to_all.44.reduce_sub_computation | reduce | bytes 8388612 | tf_op jit(solution)/shard_map/all_to_all | solution.py:76
  244.8 9.3 %reshape.304 = f32[512,1,2,16,64]{4,3,2,1,0:T(8,128)} reshape(f32[4,262144]{1,0:T(4,128)} %reduce) | data formatting | bytes 8388608
  254.1 6.9 %copy.55 = f32[2,1,16,64,4,128]{5,3,4,0,2,1:T(8,128)} copy(f32[2,1,16,64,4,128]{3,2,0,5,4,1:T(8,128)} %bitcast.154) | data formatting | bytes 8388608 | tf_op jit(solution)/shard_map/all_to_all | solution.py:76
  261.0 8.7 %convolution_bitcast_fusion.3 = f32[2,1,16,256,128]{4,3,2,0,1:T(8,128)S(1)} fusion(f32[2,16,256,128,1]{3,2,0,1,4:T(8,128)} %bitcast.155, f32[1,2,256,256]{3,2,1,0:T(8,128)S(1)} %get-tuple-element.10, f32[1,2,256,256]{3,2,1,0:T(8,128)S(1)} %get-tuple-element.9), kind=kOutput, calls=%fused_computation.12 | convolution fusion | flops 6442713088 | bytes 9437184 | tf_op jit(solution)/shard_map/itzny,oikn->otzky/dot_general | solution.py:49
  269.7 4.4 copy.56
  274.1 6.9 %all-to-all-start.1 = ((f32[2,1,16,256,128]{4,2,0,1,3:T(8,128)}), f32[2,1,16,256,128]{4,2,0,1,3:T(8,128)}, u32[]{:S(2)}, u32[]{:S(2)}) async-start(f32[2,1,16,256,128]{4,2,0,1,3:T(8,128)} %copy.56), calls=%async_computation.1 | async-start | bytes 8388608 | tf_op jit(solution)/shard_map/all_to_all | solution.py:80
  282.0 1.1 broadcast_multiply_fusion.1
  283.1 53.2 %all-to-all-done.1 = f32[2,1,16,256,128]{4,2,0,1,3:T(8,128)} async-done(((f32[2,1,16,256,128]{4,2,0,1,3:T(8,128)}), f32[2,1,16,256,128]{4,2,0,1,3:T(8,128)}, u32[]{:S(2)}, u32[]{:S(2)}) %all-to-all-start.1) | async-done | bytes 4194336 | tf_op jit(solution)/shard_map/all_to_all | solution.py:80
  336.3 2.7 copy.57
  339.1 7.1 %convolution_bitcast_fusion.2 = f32[2,256,16,128]{3,1,2,0:T(8,128)S(1)} fusion(f32[2,256,16,128,1]{3,1,0,2,4:T(8,128)S(1)} %bitcast.157, f32[1,2,256,256]{3,2,1,0:T(8,128)S(1)} %get-tuple-element.10, f32[1,2,256,256]{3,2,1,0:T(8,128)S(1)} %get-tuple-element.9), kind=kOutput, calls=%fused_computation.11 | convolution fusion | flops 6442713088 | bytes 9437184 | tf_op jit(solution)/shard_map/itnxy,oikn->otkxy/dot_general | solution.py:53
  346.2 1.5 fusion.13
  347.7 7.3 %fusion.5 = f32[2,1,256,16,128]{4,2,3,0,1:T(8,128)S(1)} fusion(f32[1,2,256,256]{3,2,1,0:T(8,128)S(1)} %get-tuple-element.8, f32[1,2,256,256]{3,2,1,0:T(8,128)S(1)} %get-tuple-element.7, f32[1,1,256,16,128]{4,2,3,1,0:T(8,128)S(1)} %get-tuple-element.6, f32[1,1,256,16,128]{4,2,3,1,0:T(8,128)S(1)} %get-tuple-element.5), kind=kOutput, calls=%fused_computation.9 | convolution fusion | flops 6443761664 | bytes 9437184 | tf_op jit(solution)/shard_map/itnxy,oikn->otkxy/dot_general | solution.py:53
  355.0 2.4 copy.64
  357.5 64.3 %all_to_all.60 = f32[2,1,256,16,128]{4,3,0,1,2:T(8,128)S(1)} all-to-all(f32[2,1,256,16,128]{4,3,0,1,2:T(8,128)S(1)} %copy.64), channel_id=1, replica_groups=mesh['sta'=2,'gx'=16,'gy'=4] {'gx'}, dimensions={2} | all-to-all | bytes 8388608 | tf_op jit(solution)/shard_map/all_to_all | solution.py:88
  422.3 6.9 %convolution_bitcast_fusion.1 = f32[2,1,16,256,128]{4,3,2,0,1:T(8,128)S(1)} fusion(f32[2,16,256,128,1]{3,2,0,1,4:T(8,128)S(1)} %bitcast.156, f32[1,2,256,256]{3,2,1,0:T(8,128)S(1)} %get-tuple-element.8, f32[1,2,256,256]{3,2,1,0:T(8,128)S(1)} %get-tuple-element.7), kind=kOutput, calls=%fused_computation.10 | convolution fusion | flops 6442713088 | bytes 9437184 | tf_op jit(solution)/shard_map/itzny,oikn->otzky/dot_general | solution.py:49
  429.2 4.4 copy.66
  433.6 5.1 all-to-all-start.3
  438.7 4.2 multiply_negate_fusion
  442.8 44.5 %all-to-all-done.3 = f32[2,1,16,256,128]{4,2,0,1,3:T(8,128)} async-done(((f32[2,1,16,256,128]{4,2,0,1,3:T(8,128)}), f32[2,1,16,256,128]{4,2,0,1,3:T(8,128)}, u32[]{:S(2)}, u32[]{:S(2)}) %all-to-all-start.3) | async-done | bytes 4194336 | tf_op jit(solution)/shard_map/all_to_all | solution.py:94
  487.3 6.9 %copy.94 = f32[2,1,16,4,64,128]{5,3,4,0,2,1:T(4,128)} copy(f32[2,1,16,4,64,128]{5,2,0,4,3,1:T(8,128)} %bitcast.57) | data formatting | bytes 8388608 | tf_op jit(solution)/shard_map/all_to_all | solution.py:94
  494.2 5.5 %reshape.274 = f32[2,16,64,512]{3,2,0,1:T(8,128)} reshape(f32[2,1,16,64,4,128]{5,4,3,0,2,1:T(4,128)} %bitcast.159) | data formatting | bytes 8388608 | tf_op jit(solution)/shard_map/reshape.27
  499.7 9.9 %fusion.19 = f32[1,16,64,512]{3,2,1,0:T(8,128)} fusion(f32[2,16,64,512]{3,2,0,1:T(8,128)} %reshape.274, f32[1,512,512]{2,1,0:T(8,128)S(1)} %get-tuple-element.17, f32[1,512,512]{2,1,0:T(8,128)S(1)} %get-tuple-element.18), kind=kOutput, calls=%fused_computation.33 | convolution fusion | flops 6442975232 | bytes 8388608 | tf_op jit(solution)/shard_map/itzxk,iyk->tzxy/dot_general | solution.py:92
  (27 shorter events, 5.6 us)
Async XLA Ops:
  6.5 1.1 copy-start
  6.5 0.8 copy-start.4
  6.5 111.5 %all-gather.2.cloned.1.call-start = ((), (), s32[]{:S(2)}) async-start(), calls=%async_computation.4 | async-start | bytes 12582912 | tf_op jit(solution)/shard_map/all_gather | solution.py:65
  7.6 16.7 %copy-start.5 = (s32[128]{0:T(128)S(1)}, s32[128]{0:T(128)}, u32[]{:S(2)}) copy-start(s32[128]{0:T(128)} %param.8) | copy-start | bytes 1540
  175.1 54.0 %all-to-all-start = ((f32[4,1,262144]{2,1,0:T(1,128)}), f32[4,1,262144]{2,1,0:T(1,128)}, u32[]{:S(2)}, u32[]{:S(2)}) async-start(f32[4,1,262144]{2,1,0:T(1,128)} %reshape.303), calls=%async_computation | async-start | bytes 8388608 | tf_op jit(solution)/shard_map/all_to_all | solution.py:76
  274.1 62.2 %all-to-all-start.1 = ((f32[2,1,16,256,128]{4,2,0,1,3:T(8,128)}), f32[2,1,16,256,128]{4,2,0,1,3:T(8,128)}, u32[]{:S(2)}, u32[]{:S(2)}) async-start(f32[2,1,16,256,128]{4,2,0,1,3:T(8,128)} %copy.56), calls=%async_computation.1 | async-start | bytes 8388608 | tf_op jit(solution)/shard_map/all_to_all | solution.py:80
  339.0 7.2 %copy-start.2 = (f32[256,16,128]{2,1,0:T(8,128)S(1)}, f32[256,16,128]{2,1,0:T(8,128)}, u32[]{:S(2)}) copy-start(f32[256,16,128]{2,1,0:T(8,128)} %param.11) | copy-start | bytes 6291460
  339.0 7.2 %copy-start.3 = (f32[256,16,128]{2,1,0:T(8,128)S(1)}, f32[256,16,128]{2,1,0:T(8,128)}, u32[]{:S(2)}) copy-start(f32[256,16,128]{2,1,0:T(8,128)} %param.10) | copy-start | bytes 6291460
  433.6 53.7 %all-to-all-start.3 = ((f32[2,1,16,256,128]{4,2,0,1,3:T(8,128)}), f32[2,1,16,256,128]{4,2,0,1,3:T(8,128)}, u32[]{:S(2)}, u32[]{:S(2)}) async-start(f32[2,1,16,256,128]{4,2,0,1,3:T(8,128)} %copy.66), calls=%async_computation.3 | async-start | bytes 8388608 | tf_op jit(solution)/shard_map/all_to_all | solution.py:94
  499.7 9.9 %copy-start.1 = (f32[128,1024]{1,0:T(8,128)S(1)}, f32[128,1024]{1,0:T(8,128)}, u32[]{:S(2)}) copy-start(f32[128,1024]{1,0:T(8,128)} %param.6) | copy-start | bytes 1572868
Sparse Core Ops, SparseCore 0:
  9.0 108.9 all-gather.1
where the time goes:
time: 526 us; the launch traced here: 517 us
  waiting for transfers between devices  235 us (45%)
  local copies, waits for them, and re-layouts  103 us (20%)
  blocking collectives  64.3 us (12%)
  matrix products  55 us (10%)
  other arithmetic  29.4 us (6%)
  starting transfers between devices  16.8 us (3%)
  between operations  13.8 us (3%)
    all_gather x1, waiting for transfers between devices, on_device(): piece = lax.all_gather(weights, 'sta', axis=0, tiled=True)  89.3 us
    all_to_all x1, blocking collectives, on_device(): lax.all_to_all(back_depth, 'gx', split_axis=2, concat_axis=3, tiled=True)  64.3 us
    all_to_all x1, waiting for transfers between devices, on_device(): lax.all_to_all(by_rows, 'gx', split_axis=3, concat_axis=2, tiled=True)  53.2 us
    all_to_all x1, waiting for transfers between devices, on_device(): lax.all_to_all(spectrum, 'gy', split_axis=4, concat_axis=3, tiled=True)  47 us
    all_to_all x1, waiting for transfers between devices, on_device(): lax.all_to_all(back_rows, 'gy', split_axis=3, concat_axis=4, tiled=True)  44.5 us
    unnamed x15, local copies, waits for them, and re-layouts  29.4 us
    gather x3, local copies, waits for them, and re-layouts, coefficients(): jnp.take_along_axis(record, positions.reshape(positions.shape[0], -1), ax...  16.8 us
    dot_general x2, matrix products, along_rows(): return jnp.einsum('itzny,oikn->otzky', piece, table, precision=HIGHEST)  15.6 us
  transfers between devices with their start and end apart: 4, of which 4 were waited for; matrix products, arithmetic and copies ran while one was open for 6% of the time, Pallas kernels for 0%

commit v1 on v0

v1 whole, which is shorter than its diff:
```python
import math

import jax
import jax.numpy as jnp
from jax import lax
from jax.sharding import PartitionSpec as P

TIMES = 2
GROUPS = 8
NOISE_POWER = 0.25
HIGHEST = lax.Precision.HIGHEST


def station_counts(station_group):
    labels = jnp.arange(GROUPS, dtype=jnp.int32)
    onehot = (station_group[:, None] == labels[None, :]).astype(jnp.float32)
    totals = jnp.sum(onehot, axis=0)
    return jnp.dot(onehot, totals, precision=HIGHEST)


def angles(rows, cols, length):
    product = rows[:, None] * cols[None, :] % length
    return product.astype(jnp.float32) * (2.0 * math.pi / length)


def local_coefficients(record, shifts, per_station):
    trace = record.shape[1]
    samples = jnp.arange(trace, dtype=jnp.int32)
    times = jnp.arange(TIMES, dtype=jnp.int32)
    positions = shifts[:, None, :] + times[None, :, None]
    hit = positions[:, :, :, None] == samples[None, None, None, :]
    values = jnp.sum(jnp.where(hit, record[:, None, None, :], 0.0), axis=3)
    scaled = values / per_station[:, None, None]
    return jnp.transpose(scaled, (1, 2, 0)).astype(jnp.bfloat16)


def on_device(record, shifts, station_group, weights, psf_real, psf_imag):
    n_sta = lax.axis_size("sta")
    n_gx = lax.axis_size("gx")
    n_gy = lax.axis_size("gy")
    k_sta = lax.axis_index("sta")
    per_station = station_counts(station_group)
    own = weights.shape[0]
    depth = shifts.shape[1]
    rows = weights.shape[1]
    width = weights.shape[2]
    nz = depth * n_gx
    nx = rows * n_gy
    cb = width // n_gy
    bb = nx // n_gx

    start = k_sta * own
    rec = lax.dynamic_slice_in_dim(record, start, own, 0)
    sh = lax.dynamic_slice_in_dim(shifts, start, own, 0)
    cnt = lax.dynamic_slice_in_dim(per_station, start, own, 0)
    coef = local_coefficients(rec, sh, cnt).reshape(TIMES * depth, own)
    partial = jnp.dot(
        coef, weights.reshape(own, rows * width), preferred_element_type=jnp.float32
    ).reshape(TIMES, depth, rows, width)
    send = lax.dynamic_index_in_dim(partial, 1 - k_sta, 0, keepdims=False)
    keep = lax.dynamic_index_in_dim(partial, k_sta, 0, keepdims=False)
    recv = lax.ppermute(send, "sta", [(i, (i + 1) % n_sta) for i in range(n_sta)])
    stack = keep + recv

    iy = jnp.arange(width, dtype=jnp.int32)
    ang_y = angles(iy, iy, width).reshape(width, n_gy, cb)
    ty = jnp.stack([jnp.cos(ang_y), -jnp.sin(ang_y)], axis=2)
    s1 = jnp.einsum("zxy,yjrc->jrzxc", stack, ty, precision=HIGHEST)
    s1 = lax.all_to_all(s1, "gy", 0, 0, tiled=True)
    s1 = s1.reshape(n_gy, 2, depth, rows, cb)

    ix = jnp.arange(nx, dtype=jnp.int32)
    ang_x = angles(ix, ix, nx)
    cx, sx = jnp.cos(ang_x), jnp.sin(ang_x)
    tx = jnp.stack([jnp.stack([cx, -sx], 1), jnp.stack([sx, cx], 1)], 0)
    tx = tx.reshape(2, n_gy, rows, 2, n_gx, bb)
    s2 = jnp.einsum("jszxc,sjxrib->irbzc", s1, tx, precision=HIGHEST)
    s2 = lax.all_to_all(s2, "gx", 0, 0, tiled=True)
    s2 = s2.reshape(n_gx, 2, bb, depth, cb)

    iz = jnp.arange(nz, dtype=jnp.int32)
    ang_z = angles(iz, iz, nz)
    cz, sz = jnp.cos(ang_z), jnp.sin(ang_z)
    tz = jnp.stack([jnp.stack([cz, -sz], 1), jnp.stack([sz, cz], 1)], 0)
    tz = tz.reshape(2, n_gx, depth, 2, nz)
    s3 = jnp.einsum("isbzc,sizra->rabc", s2, tz, precision=HIGHEST)

    power = psf_real * psf_real + psf_imag * psf_imag + NOISE_POWER
    f_re = (psf_real * s3[0] + psf_imag * s3[1]) / power
    f_im = (psf_real * s3[1] - psf_imag * s3[0]) / power
    filt = jnp.stack([f_re, f_im])

    scale_z = 1.0 / nz
    tzi = jnp.stack(
        [jnp.stack([cz, sz], 1), jnp.stack([-sz, cz], 1)], 0
    ) * scale_z
    tzi = tzi.reshape(2, nz, 2, n_gx, depth)
    g1 = jnp.einsum("sabc,sariz->irzbc", filt, tzi, precision=HIGHEST)
    g1 = lax.all_to_all(g1, "gx", 0, 0, tiled=True)
    g1 = g1.reshape(n_gx, 2, depth, bb, cb)

    scale_x = 1.0 / nx
    txi = jnp.stack(
        [jnp.stack([cx, sx], 1), jnp.stack([-sx, cx], 1)], 0
    ) * scale_x
    txi = txi.reshape(2, n_gx, bb, 2, n_gy, rows)
    g2 = jnp.einsum("iszbc,sibrjx->jrzxc", g1, txi, precision=HIGHEST)
    g2 = lax.all_to_all(g2, "gy", 0, 0, tiled=True)
    g2 = g2.reshape(n_gy, 2, depth, rows, cb)

    scale_y = 1.0 / width
    tyi = jnp.stack([jnp.cos(ang_y), -jnp.sin(ang_y)], axis=2) * scale_y
    image = jnp.einsum("jrzxc,yjrc->zxy", g2, tyi, precision=HIGHEST)
    return image[None]


def solution(mesh):
    in_specs = (
        P(),
        P(None, "gx"),
        P(),
        P("sta", "gy", None),
        P(None, "gx", "gy"),
        P(None, "gx", "gy"),
    )
    out_specs = P("sta", "gx", "gy", None)
    return jax.shard_map(
        on_device, mesh=mesh, in_specs=in_specs, out_specs=out_specs, check_vma=False
    )
```

time: 526 us -> 377 us (0.72)
  the two profiles are of different devices: /device:TPU:0 before, /device:TPU:100 now
where the time goes in v1:
time: 377 us; the launch traced here: 371 us
  waiting for transfers between devices  204 us (54%)
  matrix products  63.1 us (17%)
  blocking collectives  52.1 us (14%)
  starting transfers between devices  21 us (6%)
  other arithmetic  17.2 us (5%)
  local copies, waits for them, and re-layouts  13.4 us (4%)
    all_to_all x1, waiting for transfers between devices, on_device(): s2 = lax.all_to_all(s2, 'gx', 0, 0, tiled=True)  58.3 us
    all_to_all x1, waiting for transfers between devices, on_device(): g1 = lax.all_to_all(g1, 'gx', 0, 0, tiled=True)  58 us
    all_to_all x1, blocking collectives, on_device(): g2 = lax.all_to_all(g2, 'gy', 0, 0, tiled=True)  52.1 us
    all_to_all x1, waiting for transfers between devices, on_device(): s1 = lax.all_to_all(s1, 'gy', 0, 0, tiled=True)  45.1 us
    ppermute x1, waiting for transfers between devices, on_device(): lax.ppermute(send, 'sta', [(i, (i + 1) % n_sta) for i in range(n_sta)])  42.1 us
    dot_general x1, matrix products, on_device(): g2 = jnp.einsum('iszbc,sibrjx->jrzxc', g1, txi, precision=HIGHEST)  9.8 us
    dot_general x1, matrix products, on_device(): s2 = jnp.einsum('jszxc,sjxrib->irbzc', s1, tx, precision=HIGHEST)  9.61 us
    dot_general x1, matrix products, on_device(): s3 = jnp.einsum('isbzc,sizra->rabc', s2, tz, precision=HIGHEST)  9.43 us
  transfers between devices with their start and end apart: 4, of which 4 were waited for; matrix products, arithmetic and copies ran while one was open for 4% of the time, Pallas kernels for 0%

profile of v1, /device:TPU:100, one launch (start us, length us, event | category | flops | bytes accessed | tf_op | source)
XLA Modules:
  0.0 371.0 jit_solution(1242908851553397062)
XLA Ops:
  0.0 1.0 copy-done
  1.1 0.8 constant_dynamic-slice_fusion.3
  2.0 0.8 convert_reduce_fusion
  2.7 0.8 convolution_bitcast_fusion.1
  3.6 1.4 select_reduce_fusion
  5.1 9.4 %fusion = f32[2,16,64,512]{3,1,2,0:T(8,128)} fusion(bf16[2,16,64,1]{1,0,2,3:T(2,128)(2,1)S(1)} %fusion.88, bf16[8,8,64,512]{3,2,1,0:T(8,128)(2,1)} %bitcast.131), kind=kOutput, calls=%fused_computation.3 | convolution fusion | flops 134217728 | bytes 8392704 | tf_op jit(solution)/shard_map/dot_general | solution.py:57
  14.5 2.7 constant_dynamic-slice_fusion.1
  17.2 1.2 copy.154
  18.4 1.7 collective-permute-start
  20.2 4.1 %fusion.61 = (f32[512,4,1,128]{3,0,2,1:T(8,128)S(1)}, f32[512,4,1,128]{3,0,2,1:T(8,128)S(1)}) fusion(s32[4,128]{1,0:T(4,128)S(1)} %multiply_add_fusion.1), kind=kLoop, calls=%fused_computation.85 | loop fusion | flops 3932160 | bytes 2099200 | tf_op jit(solution)/shard_map/cos | solution.py:67
  24.3 42.1 %collective-permute-done = f32[16,64,512]{2,1,0:T(8,128)S(1)} collective-permute-done((f32[16,64,512]{2,1,0:T(8,128)S(1)}, f32[16,64,512]{2,1,0:T(8,128)S(1)}, u32[]{:S(2)}, u32[]{:S(2)}) %collective-permute-start) | collective-permute-done | bytes 2097184 | tf_op jit(solution)/shard_map/ppermute | solution.py:62
  66.3 9.3 %convolution_bitcast_fusion = f32[4,2,16,64,128]{4,3,2,1,0:T(8,128)} fusion(f32[16,64,512]{2,1,0:T(8,128)S(1)} %collective-permute-done, f32[1,16,64,512]{3,1,2,0:T(8,128)S(1)} %get-tuple-element.7, f32[512,4,1,128]{3,0,2,1:T(8,128)S(1)} %get-tuple-element.22, f32[512,4,1,128]{3,0,2,1:T(8,128)S(1)} %get-tuple-element.21), kind=kOutput, calls=%fused_computation.19 | convolution fusion | flops 6443499520 | bytes 10485760 | tf_op jit(solution)/shard_map/zxy,yjrc->jrzxc/dot_general | solution.py:68
  75.6 5.0 %all-to-all-start = ((f32[4,2,16,64,128]{4,3,2,1,0:T(8,128)}), f32[4,2,16,64,128]{4,3,2,1,0:T(8,128)}, u32[]{:S(2)}, u32[]{:S(2)}) async-start(f32[4,2,16,64,128]{4,3,2,1,0:T(8,128)} %convolution_bitcast_fusion), calls=%async_computation | async-start | bytes 8388608 | tf_op jit(solution)/shard_map/all_to_all | solution.py:69
  80.6 3.1 fusion.80
  83.8 45.1 %all-to-all-done = f32[4,2,16,64,128]{4,3,2,1,0:T(8,128)} async-done(((f32[4,2,16,64,128]{4,3,2,1,0:T(8,128)}), f32[4,2,16,64,128]{4,3,2,1,0:T(8,128)}, u32[]{:S(2)}, u32[]{:S(2)}) %all-to-all-start) | async-done | bytes 4194336 | tf_op jit(solution)/shard_map/all_to_all | solution.py:69
  128.9 9.6 %fusion.12 = f32[16,2,16,16,128]{4,2,3,0,1:T(8,128)S(1)} fusion(f32[4,2,16,64,128]{4,3,2,1,0:T(8,128)} %all-to-all-done, f32[1,4,64,1,16,16]{2,5,4,3,1,0:T(8,128)} %get-tuple-element.14, f32[1,4,64,1,16,16]{2,5,4,3,1,0:T(8,128)S(1)} %get-tuple-element.13, f32[1,4,64,1,16,16]{2,5,4,3,1,0:T(8,128)S(1)} %get-tuple-element.12), kind=kOutput, calls=%fused_computation.16 | convolution fusion | flops 6443237376 | bytes 9175040 | tf_op jit(solution)/shard_map/jszxc,sjxrib->irbzc/dot_general | solution.py:77
  138.5 3.3 copy.74
  141.8 6.9 %all-to-all-start.1 = ((f32[16,2,16,16,128]{4,3,1,2,0:T(8,128)}), f32[16,2,16,16,128]{4,3,1,2,0:T(8,128)}, u32[]{:S(2)}, u32[]{:S(2)}) async-start(f32[16,2,16,16,128]{4,3,1,2,0:T(8,128)} %copy.74), calls=%async_computation.1 | async-start | bytes 8388608 | tf_op jit(solution)/shard_map/all_to_all | solution.py:78
  148.7 1.9 fusion.86
  150.6 1.1 fusion.83
  151.7 58.3 %all-to-all-done.1 = f32[16,2,16,16,128]{4,3,1,2,0:T(8,128)} async-done(((f32[16,2,16,16,128]{4,3,1,2,0:T(8,128)}), f32[16,2,16,16,128]{4,3,1,2,0:T(8,128)}, u32[]{:S(2)}, u32[]{:S(2)}) %all-to-all-start.1) | async-done | bytes 4194336 | tf_op jit(solution)/shard_map/all_to_all | solution.py:78
  210.0 9.4 %fusion.15 = f32[2,256,16,128]{3,1,2,0:T(8,128)S(1)} fusion(f32[16,2,16,16,128]{4,3,1,2,0:T(8,128)} %all-to-all-done.1, f32[1,16,16,1,256]{4,2,0,1,3:T(8,128)} %get-tuple-element.20, f32[1,16,16,1,256]{4,2,0,1,3:T(8,128)S(1)} %get-tuple-element.19, f32[1,16,16,1,256]{4,2,0,1,3:T(8,128)S(1)} %get-tuple-element.18), kind=kOutput, calls=%fused_computation.17 | convolution fusion | flops 6443237376 | bytes 9175040 | tf_op jit(solution)/shard_map/isbzc,sizra->rabc/dot_general | solution.py:86
  219.5 1.5 divide_bitcast_fusion.1
  221.0 6.8 %fusion.21 = f32[16,2,16,16,128]{4,2,3,0,1:T(8,128)S(1)} fusion(f32[1,256,16,128]{3,1,2,0:T(8,128)S(1)} %get-tuple-element.6, f32[1,256,16,128]{3,1,2,0:T(8,128)S(1)} %get-tuple-element.5, f32[1,256,1,16,16]{1,4,3,2,0:T(8,128)S(1)} %get-tuple-element.17, f32[1,256,1,16,16]{1,4,3,2,0:T(8,128)S(1)} %get-tuple-element.16, ...), kind=kOutput, calls=%fused_computation.20 | convolution fusion | flops 6444548096 | bytes 9175040 | tf_op jit(solution)/shard_map/sabc,sariz->irzbc/dot_general | solution.py:98
  227.8 3.7 copy.85
  231.5 7.3 %all-to-all-start.2 = ((f32[16,2,16,16,128]{4,3,2,1,0:T(8,128)}), f32[16,2,16,16,128]{4,3,2,1,0:T(8,128)}, u32[]{:S(2)}, u32[]{:S(2)}) async-start(f32[16,2,16,16,128]{4,3,2,1,0:T(8,128)} %copy.85), calls=%async_computation.2 | async-start | bytes 8388608 | tf_op jit(solution)/shard_map/all_to_all | solution.py:99
  238.9 3.1 fusion.75
  242.0 58.0 %all-to-all-done.2 = f32[16,2,16,16,128]{4,3,2,1,0:T(8,128)} async-done(((f32[16,2,16,16,128]{4,3,2,1,0:T(8,128)}), f32[16,2,16,16,128]{4,3,2,1,0:T(8,128)}, u32[]{:S(2)}, u32[]{:S(2)}) %all-to-all-start.2) | async-done | bytes 4194336 | tf_op jit(solution)/shard_map/all_to_all | solution.py:99
  300.1 9.8 %fusion.18 = f32[4,2,16,64,128]{4,3,1,0,2:T(8,128)S(1)} fusion(f32[1,16,16,1,4,64]{5,2,0,1,3,4:T(8,128)} %get-tuple-element.11, f32[1,16,16,1,4,64]{5,2,0,1,3,4:T(8,128)S(1)} %get-tuple-element.10, f32[1,16,16,1,4,64]{5,2,0,1,3,4:T(8,128)S(1)} %get-tuple-element.9, f32[16,2,16,16,128]{4,3,2,1,0:T(8,128)} %all-to-all-done.2), kind=kOutput, calls=%fused_computation.18 | convolution fusion | flops 6443499520 | bytes 9175040 | tf_op jit(solution)/shard_map/iszbc,sibrjx->jrzxc/dot_general | solution.py:107
  309.9 0.6 copy.87
  310.5 52.1 %all_to_all.20 = f32[4,2,16,64,128]{4,3,1,2,0:T(8,128)S(1)} all-to-all(f32[4,2,16,64,128]{4,3,1,2,0:T(8,128)S(1)} %copy.87), channel_id=1, replica_groups=mesh['sta'=2,'gx'=16,'gy'=4] {'gy'}, dimensions={0} | all-to-all | bytes 8388608 | tf_op jit(solution)/shard_map/all_to_all | solution.py:108
  362.6 8.0 %fusion.37 = f32[1,16,64,512]{3,2,1,0:T(8,128)} fusion(f32[4,2,16,64,128]{4,3,1,2,0:T(8,128)S(1)} %all_to_all.20, f32[512,4,1,128]{3,0,2,1:T(8,128)S(1)} %get-tuple-element.22, f32[512,4,1,128]{3,0,2,1:T(8,128)S(1)} %get-tuple-element.21), kind=kOutput, calls=%fused_computation.45 | convolution fusion | flops 6443499520 | bytes 8388608 | tf_op jit(solution)/shard_map/jrzxc,yjrc->zxy/dot_general | solution.py:113
  (15 shorter events, 0.4 us)
Async XLA Ops:
  0.0 1.0 copy-start
  18.4 47.9 %collective-permute-start = (f32[16,64,512]{2,1,0:T(8,128)S(1)}, f32[16,64,512]{2,1,0:T(8,128)S(1)}, u32[]{:S(2)}, u32[]{:S(2)}) collective-permute-start(f32[16,64,512]{2,1,0:T(8,128)S(1)} %bitcast.132), channel_id=1, source_target_pairs={{0,64},{64,0},{1,65},{65,1},{2,66},{66,2},{3,67},{67,3},{4,68},{68... | collective-permute-start | bytes 6291464 | tf_op jit(solution)/shard_map/ppermute | solution.py:62
  75.6 53.3 %all-to-all-start = ((f32[4,2,16,64,128]{4,3,2,1,0:T(8,128)}), f32[4,2,16,64,128]{4,3,2,1,0:T(8,128)}, u32[]{:S(2)}, u32[]{:S(2)}) async-start(f32[4,2,16,64,128]{4,3,2,1,0:T(8,128)} %convolution_bitcast_fusion), calls=%async_computation | async-start | bytes 8388608 | tf_op jit(solution)/shard_map/all_to_all | solution.py:69
  141.8 68.2 %all-to-all-start.1 = ((f32[16,2,16,16,128]{4,3,1,2,0:T(8,128)}), f32[16,2,16,16,128]{4,3,1,2,0:T(8,128)}, u32[]{:S(2)}, u32[]{:S(2)}) async-start(f32[16,2,16,16,128]{4,3,1,2,0:T(8,128)} %copy.74), calls=%async_computation.1 | async-start | bytes 8388608 | tf_op jit(solution)/shard_map/all_to_all | solution.py:78
  210.0 9.4 %copy-start.2 = (f32[256,16,128]{2,1,0:T(8,128)S(1)}, f32[256,16,128]{2,1,0:T(8,128)}, u32[]{:S(2)}) copy-start(f32[256,16,128]{2,1,0:T(8,128)} %param.11) | copy-start | bytes 6291460
  210.0 9.5 %copy-start.3 = (f32[256,16,128]{2,1,0:T(8,128)S(1)}, f32[256,16,128]{2,1,0:T(8,128)}, u32[]{:S(2)}) copy-start(f32[256,16,128]{2,1,0:T(8,128)} %param.10) | copy-start | bytes 6291460
  231.5 68.5 %all-to-all-start.2 = ((f32[16,2,16,16,128]{4,3,2,1,0:T(8,128)}), f32[16,2,16,16,128]{4,3,2,1,0:T(8,128)}, u32[]{:S(2)}, u32[]{:S(2)}) async-start(f32[16,2,16,16,128]{4,3,2,1,0:T(8,128)} %copy.85), calls=%async_computation.2 | async-start | bytes 8388608 | tf_op jit(solution)/shard_map/all_to_all | solution.py:99
  362.6 8.0 %copy-start.1 = (f32[128,1024]{1,0:T(8,128)S(1)}, f32[128,1024]{1,0:T(8,128)}, u32[]{:S(2)}) copy-start(f32[128,1024]{1,0:T(8,128)} %param.6) | copy-start | bytes 1572868

commit v2 on v1

--- a/solution.py
+++ b/solution.py
@@ -6,9 +6,11 @@
 from jax.sharding import PartitionSpec as P
 
 TIMES = 2
+CHUNKS = 1
 GROUPS = 8
 NOISE_POWER = 0.25
 HIGHEST = lax.Precision.HIGHEST
+DFT = lax.Precision.HIGH
 
 
 def station_counts(station_group):
@@ -57,60 +59,57 @@
     partial = jnp.dot(
         coef, weights.reshape(own, rows * width), preferred_element_type=jnp.float32
     ).reshape(TIMES, depth, rows, width)
+    keep = lax.dynamic_index_in_dim(partial, k_sta, 0, keepdims=False)
     send = lax.dynamic_index_in_dim(partial, 1 - k_sta, 0, keepdims=False)
-    keep = lax.dynamic_index_in_dim(partial, k_sta, 0, keepdims=False)
-    recv = lax.ppermute(send, "sta", [(i, (i + 1) % n_sta) for i in range(n_sta)])
-    stack = keep + recv
+    pairs = [(i, (i + 1) % n_sta) for i in range(n_sta)]
+    zc = depth // CHUNKS
 
     iy = jnp.arange(width, dtype=jnp.int32)
     ang_y = angles(iy, iy, width).reshape(width, n_gy, cb)
     ty = jnp.stack([jnp.cos(ang_y), -jnp.sin(ang_y)], axis=2)
-    s1 = jnp.einsum("zxy,yjrc->jrzxc", stack, ty, precision=HIGHEST)
-    s1 = lax.all_to_all(s1, "gy", 0, 0, tiled=True)
-    s1 = s1.reshape(n_gy, 2, depth, rows, cb)
-
     ix = jnp.arange(nx, dtype=jnp.int32)
     ang_x = angles(ix, ix, nx)
     cx, sx = jnp.cos(ang_x), jnp.sin(ang_x)
     tx = jnp.stack([jnp.stack([cx, -sx], 1), jnp.stack([sx, cx], 1)], 0)
     tx = tx.reshape(2, n_gy, rows, 2, n_gx, bb)
-    s2 = jnp.einsum("jszxc,sjxrib->irbzc", s1, tx, precision=HIGHEST)
-    s2 = lax.all_to_all(s2, "gx", 0, 0, tiled=True)
-    s2 = s2.reshape(n_gx, 2, bb, depth, cb)
-
     iz = jnp.arange(nz, dtype=jnp.int32)
     ang_z = angles(iz, iz, nz)
     cz, sz = jnp.cos(ang_z), jnp.sin(ang_z)
     tz = jnp.stack([jnp.stack([cz, -sz], 1), jnp.stack([sz, cz], 1)], 0)
     tz = tz.reshape(2, n_gx, depth, 2, nz)
-    s3 = jnp.einsum("isbzc,sizra->rabc", s2, tz, precision=HIGHEST)
+
+    s3 = None
+    for k in range(CHUNKS):
+        rows_k = slice(k * zc, (k + 1) * zc)
+        recv = lax.ppermute(send[rows_k].astype(jnp.bfloat16), "sta", pairs)
+        stack = keep[rows_k] + recv.astype(jnp.float32)
+        s1 = jnp.einsum("zxy,yjrc->jrzxc", stack, ty, precision=DFT)
+        s1 = lax.all_to_all(s1, "gy", 0, 0, tiled=True)
+        s2 = jnp.einsum("jszxc,sjxrib->irbzc", s1, tx, precision=DFT)
+        s2 = lax.all_to_all(s2, "gx", 0, 0, tiled=True)
+        part = jnp.einsum("isbzc,sizra->rabc", s2, tz[:, :, rows_k], precision=DFT)
+        s3 = part if s3 is None else s3 + part
 
     power = psf_real * psf_real + psf_imag * psf_imag + NOISE_POWER
     f_re = (psf_real * s3[0] + psf_imag * s3[1]) / power
     f_im = (psf_real * s3[1] - psf_imag * s3[0]) / power
     filt = jnp.stack([f_re, f_im])
 
-    scale_z = 1.0 / nz
-    tzi = jnp.stack(
-        [jnp.stack([cz, sz], 1), jnp.stack([-sz, cz], 1)], 0
-    ) * scale_z
+    tzi = jnp.stack([jnp.stack([cz, sz], 1), jnp.stack([-sz, cz], 1)], 0) * (1.0 / nz)
     tzi = tzi.reshape(2, nz, 2, n_gx, depth)
-    g1 = jnp.einsum("sabc,sariz->irzbc", filt, tzi, precision=HIGHEST)
-    g1 = lax.all_to_all(g1, "gx", 0, 0, tiled=True)
-    g1 = g1.reshape(n_gx, 2, depth, bb, cb)
+    txi = jnp.stack([jnp.stack([cx, sx], 1), jnp.stack([-sx, cx], 1)], 0) * (1.0 / nx)
+    txi = txi.reshape(2, n_gx, bb, 2, n_gy, rows)
+    tyi = ty * (1.0 / width)
 
-    scale_x = 1.0 / nx
-    txi = jnp.stack(
-        [jnp.stack([cx, sx], 1), jnp.stack([-sx, cx], 1)], 0
-    ) * scale_x
-    txi = txi.reshape(2, n_gx, bb, 2, n_gy, rows)
-    g2 = jnp.einsum("iszbc,sibrjx->jrzxc", g1, txi, precision=HIGHEST)
-    g2 = lax.all_to_all(g2, "gy", 0, 0, tiled=True)
-    g2 = g2.reshape(n_gy, 2, depth, rows, cb)
-
-    scale_y = 1.0 / width
-    tyi = jnp.stack([jnp.cos(ang_y), -jnp.sin(ang_y)], axis=2) * scale_y
-    image = jnp.einsum("jrzxc,yjrc->zxy", g2, tyi, precision=HIGHEST)
+    pieces = []
+    for k in range(CHUNKS):
+        rows_k = slice(k * zc, (k + 1) * zc)
+        g1 = jnp.einsum("sabc,sariz->irzbc", filt, tzi[..., rows_k], precision=DFT)
+        g1 = lax.all_to_all(g1, "gx", 0, 0, tiled=True)
+        g2 = jnp.einsum("iszbc,sibrjx->jrzxc", g1, txi, precision=DFT)
+        g2 = lax.all_to_all(g2, "gy", 0, 0, tiled=True)
+        pieces.append(jnp.einsum("jrzxc,yjrc->zxy", g2, tyi, precision=DFT))
+    image = jnp.concatenate(pieces, axis=0)
     return image[None]
 
 

time: 377 us -> 330 us (0.88)
  the two profiles are of different devices: /device:TPU:100 before, /device:TPU:0 now
where the time goes in v2:
time: 330 us; the launch traced here: 325 us
  waiting for transfers between devices  169 us (51%)
  blocking collectives  51.7 us (16%)
  matrix products  43.1 us (13%)
  starting transfers between devices  27.3 us (8%)
  other arithmetic  19.5 us (6%)
  local copies, waits for them, and re-layouts  13.4 us (4%)
    all_to_all x1, waiting for transfers between devices, on_device(): s2 = lax.all_to_all(s2, 'gx', 0, 0, tiled=True)  52.5 us
    all_to_all x1, waiting for transfers between devices, on_device(): g1 = lax.all_to_all(g1, 'gx', 0, 0, tiled=True)  52.3 us
    all_to_all x1, blocking collectives, on_device(): g2 = lax.all_to_all(g2, 'gy', 0, 0, tiled=True)  51.7 us
    all_to_all x1, waiting for transfers between devices, on_device(): s1 = lax.all_to_all(s1, 'gy', 0, 0, tiled=True)  45.3 us
    ppermute x1, waiting for transfers between devices, on_device(): recv = lax.ppermute(send[rows_k].astype(jnp.bfloat16), 'sta', pairs)  19.4 us
    all_to_all x1, starting transfers between devices, on_device(): g1 = lax.all_to_all(g1, 'gx', 0, 0, tiled=True)  12.7 us
    dot_general x1, matrix products, on_device(): jnp.dot(coef, weights.reshape(own, rows * width), preferred_element_type=...  9.38 us
    all_to_all x1, starting transfers between devices, on_device(): s2 = lax.all_to_all(s2, 'gx', 0, 0, tiled=True)  7.94 us
  transfers between devices with their start and end apart: 4, of which 4 were waited for; matrix products, arithmetic and copies ran while one was open for 4% of the time, Pallas kernels for 0%

profile of v2, /device:TPU:0, one launch (start us, length us, event | category | flops | bytes accessed | tf_op | source)
XLA Modules:
  0.0 324.7 jit_solution(1845798084890678196)
XLA Ops:
  0.0 1.0 copy-done
  1.1 0.8 constant_dynamic-slice_fusion.1
  2.0 0.8 convert_reduce_fusion
  2.7 0.8 convolution_bitcast_fusion.1
  3.6 1.4 select_reduce_fusion
  5.1 9.4 %fusion = f32[2,16,64,512]{3,1,2,0:T(8,128)} fusion(bf16[2,16,64,1]{1,0,2,3:T(2,128)(2,1)S(1)} %fusion.89, bf16[8,8,64,512]{3,2,1,0:T(8,128)(2,1)} %bitcast.126), kind=kOutput, calls=%fused_computation.3 | convolution fusion | flops 134217728 | bytes 8392704 | tf_op jit(solution)/shard_map/dot_general | solution.py:59
  14.5 2.7 fusion.43
  17.2 1.6 collective-permute-start
  18.8 4.1 %fusion.62 = (f32[512,4,1,128]{3,0,2,1:T(8,128)S(1)}, f32[512,4,1,128]{3,0,2,1:T(8,128)S(1)}) fusion(s32[4,128]{1,0:T(4,128)S(1)} %multiply_add_fusion.1), kind=kLoop, calls=%fused_computation.86 | loop fusion | flops 3932160 | bytes 2099200 | tf_op jit(solution)/shard_map/cos | solution.py:69
  22.9 19.4 %collective-permute-done = bf16[16,64,512]{2,0,1:T(8,128)(2,1)} collective-permute-done((bf16[16,64,512]{2,0,1:T(8,128)(2,1)}, bf16[16,64,512]{2,0,1:T(8,128)(2,1)}, u32[]{:S(2)}, u32[]{:S(2)}) %collective-permute-start) | collective-permute-done | bytes 1048608 | tf_op jit(solution)/shard_map/ppermute | solution.py:84
  42.3 2.2 fusion.34
  44.5 5.7 %convolution_bitcast_fusion = f32[4,2,16,64,128]{4,3,2,1,0:T(8,128)} fusion(f32[16,64,512,1,1]{2,0,1,4,3:T(8,128)S(1)} %fusion.34, f32[512,4,1,128]{3,0,2,1:T(8,128)S(1)} %get-tuple-element.20, f32[512,4,1,128]{3,0,2,1:T(8,128)S(1)} %get-tuple-element.19), kind=kOutput, calls=%fused_computation.19 | convolution fusion | flops 3221749760 | bytes 8388608 | tf_op jit(solution)/shard_map/zxy,yjrc->jrzxc/dot_general | solution.py:86
  50.3 5.1 %all-to-all-start = ((f32[4,2,16,64,128]{4,3,2,1,0:T(8,128)}), f32[4,2,16,64,128]{4,3,2,1,0:T(8,128)}, u32[]{:S(2)}, u32[]{:S(2)}) async-start(f32[4,2,16,64,128]{4,3,2,1,0:T(8,128)} %convolution_bitcast_fusion), calls=%async_computation | async-start | bytes 8388608 | tf_op jit(solution)/shard_map/all_to_all | solution.py:87
  55.4 3.1 fusion.81
  58.5 45.3 %all-to-all-done = f32[4,2,16,64,128]{4,3,2,1,0:T(8,128)} async-done(((f32[4,2,16,64,128]{4,3,2,1,0:T(8,128)}), f32[4,2,16,64,128]{4,3,2,1,0:T(8,128)}, u32[]{:S(2)}, u32[]{:S(2)}) %all-to-all-start) | async-done | bytes 4194336 | tf_op jit(solution)/shard_map/all_to_all | solution.py:87
  103.8 6.2 %fusion.12 = f32[16,2,16,16,128]{4,2,0,1,3:T(8,128)S(1)} fusion(f32[4,2,16,64,128]{4,3,2,1,0:T(8,128)} %all-to-all-done, f32[1,4,64,1,16,16]{2,5,4,3,1,0:T(8,128)} %get-tuple-element.12, f32[1,4,64,1,16,16]{2,5,4,3,1,0:T(8,128)S(1)} %get-tuple-element.11, f32[1,4,64,1,16,16]{2,5,4,3,1,0:T(8,128)S(1)} %get-tuple-element.10), kind=kOutput, calls=%fused_computation.16 | convolution fusion | flops 3222011904 | bytes 9175040 | tf_op jit(solution)/shard_map/jszxc,sjxrib->irbzc/dot_general | solution.py:88
  110.0 4.4 %copy.53 = f32[16,2,16,16,128]{4,3,1,2,0:T(8,128)} copy(f32[16,2,16,16,128]{4,2,0,1,3:T(8,128)S(1)} %fusion.12) | data formatting | bytes 8388608 | tf_op jit(solution)/shard_map/jszxc,sjxrib->irbzc/transpose | solution.py:88
  114.4 7.9 %all-to-all-start.1 = ((f32[16,2,16,16,128]{4,3,1,2,0:T(8,128)}), f32[16,2,16,16,128]{4,3,1,2,0:T(8,128)}, u32[]{:S(2)}, u32[]{:S(2)}) async-start(f32[16,2,16,16,128]{4,3,1,2,0:T(8,128)} %copy.53), calls=%async_computation.1 | async-start | bytes 8388608 | tf_op jit(solution)/shard_map/all_to_all | solution.py:89
  122.4 1.9 fusion.87
  124.3 1.1 fusion.84
  125.4 52.5 %all-to-all-done.1 = f32[16,2,16,16,128]{4,3,1,2,0:T(8,128)} async-done(((f32[16,2,16,16,128]{4,3,1,2,0:T(8,128)}), f32[16,2,16,16,128]{4,3,1,2,0:T(8,128)}, u32[]{:S(2)}, u32[]{:S(2)}) %all-to-all-start.1) | async-done | bytes 4194336 | tf_op jit(solution)/shard_map/all_to_all | solution.py:89
  177.8 6.0 %fusion.15 = f32[2,256,16,128]{3,1,2,0:T(8,128)S(1)} fusion(f32[16,2,16,16,128]{4,3,1,2,0:T(8,128)} %all-to-all-done.1, f32[1,16,16,1,256]{4,2,0,1,3:T(8,128)} %get-tuple-element.18, f32[1,16,16,1,256]{4,2,0,1,3:T(8,128)S(1)} %get-tuple-element.17, f32[1,16,16,1,256]{4,2,0,1,3:T(8,128)S(1)} %get-tuple-element.16), kind=kOutput, calls=%fused_computation.17 | convolution fusion | flops 3222011904 | bytes 9175040 | tf_op jit(solution)/shard_map/isbzc,sizra->rabc/dot_general | solution.py:90
  183.9 1.5 divide_bitcast_fusion.1
  185.4 3.8 %fusion.21 = f32[16,2,16,16,128]{4,2,3,0,1:T(8,128)S(1)} fusion(f32[1,256,16,128]{3,1,2,0:T(8,128)S(1)} %get-tuple-element.6, f32[1,256,16,128]{3,1,2,0:T(8,128)S(1)} %get-tuple-element.5, f32[1,256,1,16,16]{1,4,3,2,0:T(8,128)S(1)} %get-tuple-element.15, f32[1,256,1,16,16]{1,4,3,2,0:T(8,128)S(1)} %get-tuple-element.14, ...), kind=kOutput, calls=%fused_computation.20 | convolution fusion | flops 3223322624 | bytes 9175040 | tf_op jit(solution)/shard_map/sabc,sariz->irzbc/dot_general | solution.py:107
  189.2 3.7 %copy.64 = f32[16,2,16,16,128]{4,3,2,1,0:T(8,128)} copy(f32[16,2,16,16,128]{4,2,3,0,1:T(8,128)S(1)} %fusion.21) | data formatting | bytes 8388608 | tf_op jit(solution)/shard_map/sabc,sariz->irzbc/transpose | solution.py:107
  192.9 12.7 %all-to-all-start.2 = ((f32[16,2,16,16,128]{4,3,2,1,0:T(8,128)}), f32[16,2,16,16,128]{4,3,2,1,0:T(8,128)}, u32[]{:S(2)}, u32[]{:S(2)}) async-start(f32[16,2,16,16,128]{4,3,2,1,0:T(8,128)} %copy.64), calls=%async_computation.2 | async-start | bytes 8388608 | tf_op jit(solution)/shard_map/all_to_all | solution.py:108
  205.6 3.1 fusion.76
  208.8 52.3 %all-to-all-done.2 = f32[16,2,16,16,128]{4,3,2,1,0:T(8,128)} async-done(((f32[16,2,16,16,128]{4,3,2,1,0:T(8,128)}), f32[16,2,16,16,128]{4,3,2,1,0:T(8,128)}, u32[]{:S(2)}, u32[]{:S(2)}) %all-to-all-start.2) | async-done | bytes 4194336 | tf_op jit(solution)/shard_map/all_to_all | solution.py:108
  261.1 6.4 %fusion.18 = f32[4,2,16,64,128]{4,3,1,0,2:T(8,128)S(1)} fusion(f32[1,16,16,1,4,64]{5,2,0,1,3,4:T(8,128)} %get-tuple-element.9, f32[1,16,16,1,4,64]{5,2,0,1,3,4:T(8,128)S(1)} %get-tuple-element.8, f32[1,16,16,1,4,64]{5,2,0,1,3,4:T(8,128)S(1)} %get-tuple-element.7, f32[16,2,16,16,128]{4,3,2,1,0:T(8,128)} %all-to-all-done.2), kind=kOutput, calls=%fused_computation.18 | convolution fusion | flops 3222274048 | bytes 9175040 | tf_op jit(solution)/shard_map/iszbc,sibrjx->jrzxc/dot_general | solution.py:109
  267.5 0.6 copy.66
  268.1 51.7 %all_to_all.20 = f32[4,2,16,64,128]{4,3,1,2,0:T(8,128)S(1)} all-to-all(f32[4,2,16,64,128]{4,3,1,2,0:T(8,128)S(1)} %copy.66), channel_id=1, replica_groups=mesh['sta'=2,'gx'=16,'gy'=4] {'gy'}, dimensions={0} | all-to-all | bytes 8388608 | tf_op jit(solution)/shard_map/all_to_all | solution.py:110
  319.8 4.8 %fusion.37 = f32[1,16,64,512]{3,2,1,0:T(8,128)} fusion(f32[4,2,16,64,128]{4,3,1,2,0:T(8,128)S(1)} %all_to_all.20, f32[512,4,1,128]{3,0,2,1:T(8,128)S(1)} %get-tuple-element.20, f32[512,4,1,128]{3,0,2,1:T(8,128)S(1)} %get-tuple-element.19), kind=kOutput, calls=%fused_computation.45 | convolution fusion | flops 3222274048 | bytes 8388608 | tf_op jit(solution)/shard_map/jrzxc,yjrc->zxy/dot_general | solution.py:111
  (15 shorter events, 0.4 us)
Async XLA Ops:
  0.0 1.0 copy-start
  17.2 25.0 %collective-permute-start = (bf16[16,64,512]{2,0,1:T(8,128)(2,1)}, bf16[16,64,512]{2,0,1:T(8,128)(2,1)}, u32[]{:S(2)}, u32[]{:S(2)}) collective-permute-start(bf16[16,64,512]{2,0,1:T(8,128)(2,1)} %fusion.43), channel_id=1, source_target_pairs={{0,64},{64,0},{1,65},{65,1},{2,66},{66,2},{3,67},{67,3},{4,68},{68... | collective-permute-start | bytes 3145736 | tf_op jit(solution)/shard_map/ppermute | solution.py:84
  50.3 53.6 %all-to-all-start = ((f32[4,2,16,64,128]{4,3,2,1,0:T(8,128)}), f32[4,2,16,64,128]{4,3,2,1,0:T(8,128)}, u32[]{:S(2)}, u32[]{:S(2)}) async-start(f32[4,2,16,64,128]{4,3,2,1,0:T(8,128)} %convolution_bitcast_fusion), calls=%async_computation | async-start | bytes 8388608 | tf_op jit(solution)/shard_map/all_to_all | solution.py:87
  114.4 63.4 %all-to-all-start.1 = ((f32[16,2,16,16,128]{4,3,1,2,0:T(8,128)}), f32[16,2,16,16,128]{4,3,1,2,0:T(8,128)}, u32[]{:S(2)}, u32[]{:S(2)}) async-start(f32[16,2,16,16,128]{4,3,1,2,0:T(8,128)} %copy.53), calls=%async_computation.1 | async-start | bytes 8388608 | tf_op jit(solution)/shard_map/all_to_all | solution.py:89
  177.8 6.0 %copy-start.2 = (f32[256,16,128]{2,1,0:T(8,128)S(1)}, f32[256,16,128]{2,1,0:T(8,128)}, u32[]{:S(2)}) copy-start(f32[256,16,128]{2,1,0:T(8,128)} %param.11) | copy-start | bytes 6291460
  177.8 6.0 %copy-start.3 = (f32[256,16,128]{2,1,0:T(8,128)S(1)}, f32[256,16,128]{2,1,0:T(8,128)}, u32[]{:S(2)}) copy-start(f32[256,16,128]{2,1,0:T(8,128)} %param.10) | copy-start | bytes 6291460
  192.9 68.2 %all-to-all-start.2 = ((f32[16,2,16,16,128]{4,3,2,1,0:T(8,128)}), f32[16,2,16,16,128]{4,3,2,1,0:T(8,128)}, u32[]{:S(2)}, u32[]{:S(2)}) async-start(f32[16,2,16,16,128]{4,3,2,1,0:T(8,128)} %copy.64), calls=%async_computation.2 | async-start | bytes 8388608 | tf_op jit(solution)/shard_map/all_to_all | solution.py:108
  319.8 4.8 %copy-start.1 = (f32[128,1024]{1,0:T(8,128)S(1)}, f32[128,1024]{1,0:T(8,128)}, u32[]{:S(2)}) copy-start(f32[128,1024]{1,0:T(8,128)} %param.6) | copy-start | bytes 1572868

commit v3 on v2

--- a/solution.py
+++ b/solution.py
@@ -105,7 +105,8 @@
     for k in range(CHUNKS):
         rows_k = slice(k * zc, (k + 1) * zc)
         g1 = jnp.einsum("sabc,sariz->irzbc", filt, tzi[..., rows_k], precision=DFT)
-        g1 = lax.all_to_all(g1, "gx", 0, 0, tiled=True)
+        g1 = lax.all_to_all(g1.astype(jnp.bfloat16), "gx", 0, 0, tiled=True)
+        g1 = g1.astype(jnp.float32)
         g2 = jnp.einsum("iszbc,sibrjx->jrzxc", g1, txi, precision=DFT)
         g2 = lax.all_to_all(g2, "gy", 0, 0, tiled=True)
         pieces.append(jnp.einsum("jrzxc,yjrc->zxy", g2, tyi, precision=DFT))

time: 330 us -> 292 us (0.88); the launches traced: 325 us -> 291 us
  waiting for transfers between devices: 169 us -> 145 us
  matrix products: 43.1 us -> 39.4 us
    all_to_all x1, waiting for transfers between devices: 52.3 us -> 26.1 us  [on_device(): g1 = lax.all_to_all(g1.astype(jnp.bfloat16), 'gx', 0, 0, tiled=True)]
    transpose x1 -> x0, local copies, waits for them, and re-layouts: 3.7 us -> none  [on_device(): g1 = jnp.einsum('sabc,sariz->irzbc', filt, tzi[..., rows_k], precision=DFT)]
where the time goes in v3:
time: 292 us; the launch traced here: 291 us
  waiting for transfers between devices  145 us (50%)
  blocking collectives  51.5 us (18%)
  matrix products  39.4 us (13%)
  starting transfers between devices  27.5 us (9%)
  other arithmetic  17.4 us (6%)
  local copies, waits for them, and re-layouts  10.6 us (4%)
    all_to_all x1, waiting for transfers between devices, on_device(): s2 = lax.all_to_all(s2, 'gx', 0, 0, tiled=True)  53.2 us
    all_to_all x1, blocking collectives, on_device(): g2 = lax.all_to_all(g2, 'gy', 0, 0, tiled=True)  51.5 us
    all_to_all x1, waiting for transfers between devices, on_device(): s1 = lax.all_to_all(s1, 'gy', 0, 0, tiled=True)  46.3 us
    all_to_all x1, waiting for transfers between devices, on_device(): g1 = lax.all_to_all(g1.astype(jnp.bfloat16), 'gx', 0, 0, tiled=True)  26.1 us
    ppermute x1, waiting for transfers between devices, on_device(): recv = lax.ppermute(send[rows_k].astype(jnp.bfloat16), 'sta', pairs)  19 us
    all_to_all x1, starting transfers between devices, on_device(): g1 = lax.all_to_all(g1.astype(jnp.bfloat16), 'gx', 0, 0, tiled=True)  12.7 us
    dot_general x1, matrix products, on_device(): jnp.dot(coef, weights.reshape(own, rows * width), preferred_element_type=...  9.38 us
    all_to_all x1, starting transfers between devices, on_device(): s2 = lax.all_to_all(s2, 'gx', 0, 0, tiled=True)  7.94 us
  transfers between devices with their start and end apart: 4, of which 4 were waited for; matrix products, arithmetic and copies ran while one was open for 4% of the time, Pallas kernels for 0%

profile of v3, /device:TPU:0, one launch (start us, length us, event | category | flops | bytes accessed | tf_op | source)
XLA Modules:
  0.0 291.3 jit_solution(13756137992951881636)
XLA Ops:
  0.0 1.0 copy-done
  1.1 0.8 constant_dynamic-slice_fusion.1
  2.0 0.8 convert_reduce_fusion
  2.7 0.8 convolution_bitcast_fusion.2
  3.6 1.4 select_reduce_fusion
  5.1 9.4 %fusion = f32[2,16,64,512]{3,1,2,0:T(8,128)} fusion(bf16[2,16,64,1]{1,0,2,3:T(2,128)(2,1)S(1)} %fusion.85, bf16[8,8,64,512]{3,2,1,0:T(8,128)(2,1)} %bitcast.128), kind=kOutput, calls=%fused_computation.3 | convolution fusion | flops 134217728 | bytes 8392704 | tf_op jit(solution)/shard_map/dot_general | solution.py:59
  14.5 1.8 fusion.39
  16.3 1.8 collective-permute-start
  18.1 4.1 %fusion.58 = (f32[512,4,1,128]{3,0,2,1:T(8,128)S(1)}, f32[512,4,1,128]{3,0,2,1:T(8,128)S(1)}) fusion(s32[4,128]{1,0:T(4,128)S(1)} %multiply_add_fusion.1), kind=kLoop, calls=%fused_computation.86 | loop fusion | flops 3932160 | bytes 2099200 | tf_op jit(solution)/shard_map/cos | solution.py:69
  22.2 19.0 %collective-permute-done = bf16[16,64,512]{2,0,1:T(8,128)(2,1)S(1)} collective-permute-done((bf16[16,64,512]{2,0,1:T(8,128)(2,1)S(1)}, bf16[16,64,512]{2,0,1:T(8,128)(2,1)S(1)}, u32[]{:S(2)}, u32[]{:S(2)}) %collective-permute-start) | collective-permute-done | bytes 1048608 | tf_op jit(solution)/shard_map/ppermute | solution.py:84
  41.3 1.9 fusion.30
  43.2 5.7 %convolution_bitcast_fusion.1 = f32[4,2,16,64,128]{4,3,2,1,0:T(8,128)} fusion(f32[16,64,512,1,1]{2,0,1,4,3:T(8,128)S(1)} %fusion.30, f32[512,4,1,128]{3,0,2,1:T(8,128)S(1)} %get-tuple-element.20, f32[512,4,1,128]{3,0,2,1:T(8,128)S(1)} %get-tuple-element.19), kind=kOutput, calls=%fused_computation.18 | convolution fusion | flops 3221749760 | bytes 8388608 | tf_op jit(solution)/shard_map/zxy,yjrc->jrzxc/dot_general | solution.py:86
  48.9 5.1 %all-to-all-start = ((f32[4,2,16,64,128]{4,3,2,1,0:T(8,128)}), f32[4,2,16,64,128]{4,3,2,1,0:T(8,128)}, u32[]{:S(2)}, u32[]{:S(2)}) async-start(f32[4,2,16,64,128]{4,3,2,1,0:T(8,128)} %convolution_bitcast_fusion.1), calls=%async_computation | async-start | bytes 8388608 | tf_op jit(solution)/shard_map/all_to_all | solution.py:87
  54.0 2.1 fusion.77
  56.1 46.3 %all-to-all-done = f32[4,2,16,64,128]{4,3,2,1,0:T(8,128)} async-done(((f32[4,2,16,64,128]{4,3,2,1,0:T(8,128)}), f32[4,2,16,64,128]{4,3,2,1,0:T(8,128)}, u32[]{:S(2)}, u32[]{:S(2)}) %all-to-all-start) | async-done | bytes 4194336 | tf_op jit(solution)/shard_map/all_to_all | solution.py:87
  102.4 5.5 %fusion.10 = f32[16,2,16,16,128]{4,2,0,1,3:T(8,128)S(1)} fusion(f32[4,2,16,64,128]{4,3,2,1,0:T(8,128)} %all-to-all-done, f32[1,4,64,1,16,16]{2,5,4,3,1,0:T(8,128)S(1)} %get-tuple-element.9, f32[1,4,64,1,16,16]{2,5,4,3,1,0:T(8,128)S(1)} %get-tuple-element.8, f32[1,4,64,1,16,16]{2,5,4,3,1,0:T(8,128)S(1)} %get-tuple-element.7), kind=kOutput, calls=%fused_computation.15 | convolution fusion | flops 3222011904 | bytes 9175040 | tf_op jit(solution)/shard_map/jszxc,sjxrib->irbzc/dot_general | solution.py:88
  107.9 4.4 %copy.53 = f32[16,2,16,16,128]{4,3,1,2,0:T(8,128)} copy(f32[16,2,16,16,128]{4,2,0,1,3:T(8,128)S(1)} %fusion.10) | data formatting | bytes 8388608 | tf_op jit(solution)/shard_map/jszxc,sjxrib->irbzc/transpose | solution.py:88
  112.3 7.9 %all-to-all-start.1 = ((f32[16,2,16,16,128]{4,3,1,2,0:T(8,128)}), f32[16,2,16,16,128]{4,3,1,2,0:T(8,128)}, u32[]{:S(2)}, u32[]{:S(2)}) async-start(f32[16,2,16,16,128]{4,3,1,2,0:T(8,128)} %copy.53), calls=%async_computation.1 | async-start | bytes 8388608 | tf_op jit(solution)/shard_map/all_to_all | solution.py:89
  120.3 1.1 fusion.83
  121.4 1.1 fusion.80
  122.5 53.2 %all-to-all-done.1 = f32[16,2,16,16,128]{4,3,1,2,0:T(8,128)} async-done(((f32[16,2,16,16,128]{4,3,1,2,0:T(8,128)}), f32[16,2,16,16,128]{4,3,1,2,0:T(8,128)}, u32[]{:S(2)}, u32[]{:S(2)}) %all-to-all-start.1) | async-done | bytes 4194336 | tf_op jit(solution)/shard_map/all_to_all | solution.py:89
  175.7 5.6 %fusion.13 = f32[2,256,16,128]{3,1,2,0:T(8,128)S(1)} fusion(f32[16,2,16,16,128]{4,3,1,2,0:T(8,128)} %all-to-all-done.1, f32[1,16,16,1,256]{4,2,0,1,3:T(8,128)S(1)} %get-tuple-element.18, f32[1,16,16,1,256]{4,2,0,1,3:T(8,128)S(1)} %get-tuple-element.17, f32[1,16,16,1,256]{4,2,0,1,3:T(8,128)S(1)} %get-tuple-element.16), kind=kOutput, calls=%fused_computation.16 | convolution fusion | flops 3222011904 | bytes 9175040 | tf_op jit(solution)/shard_map/isbzc,sizra->rabc/dot_general | solution.py:90
  181.3 1.5 divide_bitcast_fusion.1
  182.8 3.9 %fusion.16 = bf16[16,2,16,16,128]{4,2,3,0,1:T(8,128)(2,1)S(1)} fusion(f32[1,256,16,128]{3,1,2,0:T(8,128)S(1)} %get-tuple-element.6, f32[1,256,16,128]{3,1,2,0:T(8,128)S(1)} %get-tuple-element.5, f32[1,256,1,16,16]{1,4,3,2,0:T(8,128)S(1)} %get-tuple-element.15, f32[1,256,1,16,16]{1,4,3,2,0:T(8,128)S(1)} %get-tuple-element.14, ...), kind=kOutput, calls=%fused_computation.19 | convolution fusion | flops 3224371200 | bytes 7077888 | tf_op jit(solution)/shard_map/sabc,sariz->irzbc/dot_general | solution.py:107
  186.8 1.9 copy.64
  188.6 12.7 %all-to-all-start.2 = ((bf16[16,2,16,16,128]{4,3,2,1,0:T(8,128)(2,1)}), bf16[16,2,16,16,128]{4,3,2,1,0:T(8,128)(2,1)S(1)}, u32[]{:S(2)}, u32[]{:S(2)}) async-start(bf16[16,2,16,16,128]{4,3,2,1,0:T(8,128)(2,1)} %copy.64), calls=%async_computation.2 | async-start | bytes 4194304 | tf_op jit(solution)/shard_map/all_to_all | solution.py:108
  201.3 3.2 %fusion.72 = (f32[1,16,16,1,4,64]{5,2,0,1,3,4:T(8,128)S(1)}, f32[1,16,16,1,4,64]{5,2,0,1,3,4:T(8,128)S(1)}, f32[1,16,16,1,4,64]{5,2,0,1,3,4:T(8,128)}) fusion(s32[4,64]{1,0:T(4,128)S(1)} %multiply_add_fusion.2, s32[16,16]{1,0:T(8,128)S(1)} %multiply_add_fusion), kind=kLoop, calls=%fused_computation.106 | loop fusion | flops 983040 | bytes 788480 | tf_op jit(solution)/shard_map/sin | solution.py:72
  204.5 26.1 %all-to-all-done.2 = bf16[16,2,16,16,128]{4,3,2,1,0:T(8,128)(2,1)S(1)} async-done(((bf16[16,2,16,16,128]{4,3,2,1,0:T(8,128)(2,1)}), bf16[16,2,16,16,128]{4,3,2,1,0:T(8,128)(2,1)S(1)}, u32[]{:S(2)}, u32[]{:S(2)}) %all-to-all-start.2) | async-done | bytes 2097184 | tf_op jit(solution)/shard_map/all_to_all | solution.py:108
  230.6 3.8 %convolution_bitcast_fusion = f32[4,2,16,64,128]{4,3,1,0,2:T(8,128)S(1)} fusion(f32[1,16,16,1,4,64]{5,2,0,1,3,4:T(8,128)} %get-tuple-element.12, f32[1,16,16,1,4,64]{5,2,0,1,3,4:T(8,128)S(1)} %get-tuple-element.11, f32[1,16,16,1,4,64]{5,2,0,1,3,4:T(8,128)S(1)} %get-tuple-element.10, bf16[16,2,16,16,128]{4,3,2,1,0:T(8,128)(2,1)S(1)} %all-to-all-done.2), kind=kOutput, calls=%fused_computation.17 | convolution fusion | flops 3222274048 | bytes 7077888 | tf_op jit(solution)/shard_map/iszbc,sibrjx->jrzxc/dot_general | solution.py:110
  234.4 0.6 copy.66
  235.0 51.5 %all_to_all.20 = f32[4,2,16,64,128]{4,3,1,2,0:T(8,128)S(1)} all-to-all(f32[4,2,16,64,128]{4,3,1,2,0:T(8,128)S(1)} %copy.66), channel_id=1, replica_groups=mesh['sta'=2,'gx'=16,'gy'=4] {'gy'}, dimensions={0} | all-to-all | bytes 8388608 | tf_op jit(solution)/shard_map/all_to_all | solution.py:111
  286.5 4.8 %fusion.33 = f32[1,16,64,512]{3,2,1,0:T(8,128)} fusion(f32[4,2,16,64,128]{4,3,1,2,0:T(8,128)S(1)} %all_to_all.20, f32[512,4,1,128]{3,0,2,1:T(8,128)S(1)} %copy-done.5, f32[512,4,1,128]{3,0,2,1:T(8,128)S(1)} %copy-done.3), kind=kOutput, calls=%fused_computation.45 | convolution fusion | flops 3222274048 | bytes 8388608 | tf_op jit(solution)/shard_map/jrzxc,yjrc->zxy/dot_general | solution.py:112
  (23 shorter events, 0.4 us)
Async XLA Ops:
  0.0 1.0 copy-start
  16.3 25.0 %collective-permute-start = (bf16[16,64,512]{2,0,1:T(8,128)(2,1)S(1)}, bf16[16,64,512]{2,0,1:T(8,128)(2,1)S(1)}, u32[]{:S(2)}, u32[]{:S(2)}) collective-permute-start(bf16[16,64,512]{2,0,1:T(8,128)(2,1)S(1)} %fusion.39), channel_id=1, source_target_pairs={{0,64},{64,0},{1,65},{65,1},{2,66},{66,2},{3,67},{67,3},{4,68},{68... | collective-permute-start | bytes 3145736 | tf_op jit(solution)/shard_map/ppermute | solution.py:84
  22.2 21.0 %copy-start.2 = (f32[512,4,1,128]{3,0,2,1:T(8,128)}, f32[512,4,1,128]{3,0,2,1:T(8,128)S(1)}, u32[]{:S(2)}) copy-start(f32[512,4,1,128]{3,0,2,1:T(8,128)S(1)} %get-tuple-element.19) | copy-start | bytes 3145732
  22.2 21.0 %copy-start.4 = (f32[512,4,1,128]{3,0,2,1:T(8,128)}, f32[512,4,1,128]{3,0,2,1:T(8,128)S(1)}, u32[]{:S(2)}) copy-start(f32[512,4,1,128]{3,0,2,1:T(8,128)S(1)} %get-tuple-element.20) | copy-start | bytes 3145732
  48.9 53.5 %all-to-all-start = ((f32[4,2,16,64,128]{4,3,2,1,0:T(8,128)}), f32[4,2,16,64,128]{4,3,2,1,0:T(8,128)}, u32[]{:S(2)}, u32[]{:S(2)}) async-start(f32[4,2,16,64,128]{4,3,2,1,0:T(8,128)} %convolution_bitcast_fusion.1), calls=%async_computation | async-start | bytes 8388608 | tf_op jit(solution)/shard_map/all_to_all | solution.py:87
  112.3 63.4 %all-to-all-start.1 = ((f32[16,2,16,16,128]{4,3,1,2,0:T(8,128)}), f32[16,2,16,16,128]{4,3,1,2,0:T(8,128)}, u32[]{:S(2)}, u32[]{:S(2)}) async-start(f32[16,2,16,16,128]{4,3,1,2,0:T(8,128)} %copy.53), calls=%async_computation.1 | async-start | bytes 8388608 | tf_op jit(solution)/shard_map/all_to_all | solution.py:89
  175.7 5.6 %copy-start.6 = (f32[256,16,128]{2,1,0:T(8,128)S(1)}, f32[256,16,128]{2,1,0:T(8,128)}, u32[]{:S(2)}) copy-start(f32[256,16,128]{2,1,0:T(8,128)} %param.11) | copy-start | bytes 6291460
  175.7 5.6 %copy-start.7 = (f32[256,16,128]{2,1,0:T(8,128)S(1)}, f32[256,16,128]{2,1,0:T(8,128)}, u32[]{:S(2)}) copy-start(f32[256,16,128]{2,1,0:T(8,128)} %param.10) | copy-start | bytes 6291460
  188.6 42.0 %all-to-all-start.2 = ((bf16[16,2,16,16,128]{4,3,2,1,0:T(8,128)(2,1)}), bf16[16,2,16,16,128]{4,3,2,1,0:T(8,128)(2,1)S(1)}, u32[]{:S(2)}, u32[]{:S(2)}) async-start(bf16[16,2,16,16,128]{4,3,2,1,0:T(8,128)(2,1)} %copy.64), calls=%async_computation.2 | async-start | bytes 4194304 | tf_op jit(solution)/shard_map/all_to_all | solution.py:108
  235.0 51.6 %copy-start.3 = (f32[512,4,1,128]{3,0,2,1:T(8,128)S(1)}, f32[512,4,1,128]{3,0,2,1:T(8,128)}, u32[]{:S(2)}) copy-start(f32[512,4,1,128]{3,0,2,1:T(8,128)} %copy-done.2) | copy-start | bytes 3145732
  235.0 51.5 %copy-start.5 = (f32[512,4,1,128]{3,0,2,1:T(8,128)S(1)}, f32[512,4,1,128]{3,0,2,1:T(8,128)}, u32[]{:S(2)}) copy-start(f32[512,4,1,128]{3,0,2,1:T(8,128)} %copy-done.4) | copy-start | bytes 3145732
  235.0 56.3 %copy-start.1 = (f32[128,1024]{1,0:T(8,128)S(1)}, f32[128,1024]{1,0:T(8,128)}, u32[]{:S(2)}) copy-start(f32[128,1024]{1,0:T(8,128)} %param.6) | copy-start | bytes 1572868

commit v4 on v2

--- a/solution.py
+++ b/solution.py
@@ -7,6 +7,7 @@
 
 TIMES = 2
 CHUNKS = 1
+LINK_INV_Z = None
 GROUPS = 8
 NOISE_POWER = 0.25
 HIGHEST = lax.Precision.HIGHEST
@@ -36,11 +37,36 @@
     return jnp.transpose(scaled, (1, 2, 0)).astype(jnp.bfloat16)
 
 
+def exchange(pieces, axis, n, link=None):
+    out = [pieces[0]]
+    for d in range(1, n):
+        piece = pieces[d] if link is None else pieces[d].astype(link)
+        got = lax.ppermute(piece, axis, [(s, (s + d) % n) for s in range(n)])
+        out.append(got if link is None else got.astype(pieces.dtype))
+    return jnp.stack(out)
+
+
+def block_index(me, n, size, sign):
+    d = jnp.arange(n, dtype=jnp.int32)[:, None]
+    t = jnp.arange(size, dtype=jnp.int32)[None, :]
+    return (((me + sign * d) % n) * size + t).reshape(-1)
+
+
+def complex_block(rows, cols, length, sign, scale):
+    ang = angles(rows, cols, length)
+    cos, sin = jnp.cos(ang) * scale, jnp.sin(ang) * scale
+    if sign < 0:
+        return jnp.stack([jnp.stack([cos, -sin], 1), jnp.stack([sin, cos], 1)], 0)
+    return jnp.stack([jnp.stack([cos, sin], 1), jnp.stack([-sin, cos], 1)], 0)
+
+
 def on_device(record, shifts, station_group, weights, psf_real, psf_imag):
     n_sta = lax.axis_size("sta")
     n_gx = lax.axis_size("gx")
     n_gy = lax.axis_size("gy")
     k_sta = lax.axis_index("sta")
+    k_gx = lax.axis_index("gx")
+    k_gy = lax.axis_index("gy")
     per_station = station_counts(station_group)
     own = weights.shape[0]
     depth = shifts.shape[1]
@@ -65,17 +91,13 @@
     zc = depth // CHUNKS
 
     iy = jnp.arange(width, dtype=jnp.int32)
-    ang_y = angles(iy, iy, width).reshape(width, n_gy, cb)
+    iz = jnp.arange(nz, dtype=jnp.int32)
+    ang_y = angles(iy, block_index(k_gy, n_gy, cb, 1), width).reshape(width, n_gy, cb)
     ty = jnp.stack([jnp.cos(ang_y), -jnp.sin(ang_y)], axis=2)
-    ix = jnp.arange(nx, dtype=jnp.int32)
-    ang_x = angles(ix, ix, nx)
-    cx, sx = jnp.cos(ang_x), jnp.sin(ang_x)
-    tx = jnp.stack([jnp.stack([cx, -sx], 1), jnp.stack([sx, cx], 1)], 0)
-    tx = tx.reshape(2, n_gy, rows, 2, n_gx, bb)
-    iz = jnp.arange(nz, dtype=jnp.int32)
-    ang_z = angles(iz, iz, nz)
-    cz, sz = jnp.cos(ang_z), jnp.sin(ang_z)
-    tz = jnp.stack([jnp.stack([cz, -sz], 1), jnp.stack([sz, cz], 1)], 0)
+    tx = complex_block(
+        block_index(k_gy, n_gy, rows, -1), block_index(k_gx, n_gx, bb, 1), nx, -1, 1.0
+    ).reshape(2, n_gy, rows, 2, n_gx, bb)
+    tz = complex_block(block_index(k_gx, n_gx, depth, -1), iz, nz, -1, 1.0)
     tz = tz.reshape(2, n_gx, depth, 2, nz)
 
     s3 = None
@@ -83,10 +105,10 @@
         rows_k = slice(k * zc, (k + 1) * zc)
         recv = lax.ppermute(send[rows_k].astype(jnp.bfloat16), "sta", pairs)
         stack = keep[rows_k] + recv.astype(jnp.float32)
-        s1 = jnp.einsum("zxy,yjrc->jrzxc", stack, ty, precision=DFT)
-        s1 = lax.all_to_all(s1, "gy", 0, 0, tiled=True)
+        s1 = jnp.einsum("zxy,ydrc->drzxc", stack, ty, precision=DFT)
+        s1 = exchange(s1, "gy", n_gy)
         s2 = jnp.einsum("jszxc,sjxrib->irbzc", s1, tx, precision=DFT)
-        s2 = lax.all_to_all(s2, "gx", 0, 0, tiled=True)
+        s2 = exchange(s2, "gx", n_gx)
         part = jnp.einsum("isbzc,sizra->rabc", s2, tz[:, :, rows_k], precision=DFT)
         s3 = part if s3 is None else s3 + part
 
@@ -95,21 +117,23 @@
     f_im = (psf_real * s3[1] - psf_imag * s3[0]) / power
     filt = jnp.stack([f_re, f_im])
 
-    tzi = jnp.stack([jnp.stack([cz, sz], 1), jnp.stack([-sz, cz], 1)], 0) * (1.0 / nz)
+    tzi = complex_block(iz, block_index(k_gx, n_gx, depth, 1), nz, 1, 1.0 / nz)
     tzi = tzi.reshape(2, nz, 2, n_gx, depth)
-    txi = jnp.stack([jnp.stack([cx, sx], 1), jnp.stack([-sx, cx], 1)], 0) * (1.0 / nx)
-    txi = txi.reshape(2, n_gx, bb, 2, n_gy, rows)
-    tyi = ty * (1.0 / width)
+    txi = complex_block(
+        block_index(k_gx, n_gx, bb, -1), block_index(k_gy, n_gy, rows, 1), nx, 1, 1.0 / nx
+    ).reshape(2, n_gx, bb, 2, n_gy, rows)
+    ang_yi = angles(block_index(k_gy, n_gy, cb, -1), iy, width).reshape(n_gy, cb, width)
+    tyi = jnp.stack([jnp.cos(ang_yi), -jnp.sin(ang_yi)], axis=1) * (1.0 / width)
 
     pieces = []
     for k in range(CHUNKS):
         rows_k = slice(k * zc, (k + 1) * zc)
         g1 = jnp.einsum("sabc,sariz->irzbc", filt, tzi[..., rows_k], precision=DFT)
-        g1 = lax.all_to_all(g1, "gx", 0, 0, tiled=True)
+        g1 = exchange(g1, "gx", n_gx, LINK_INV_Z)
         g2 = jnp.einsum("iszbc,sibrjx->jrzxc", g1, txi, precision=DFT)
-        g2 = lax.all_to_all(g2, "gy", 0, 0, tiled=True)
-        pieces.append(jnp.einsum("jrzxc,yjrc->zxy", g2, tyi, precision=DFT))
-    image = jnp.concatenate(pieces, axis=0)
+        g2 = exchange(g2, "gy", n_gy)
+        pieces.append(jnp.einsum("jrzxc,jrcy->zxy", g2, tyi, precision=DFT))
+    image = jnp.concatenate(pieces, axis=0) if CHUNKS > 1 else pieces[0]
     return image[None]
 
 

time: 330 us -> 337 us (1.021)
  starting transfers between devices: 27.3 us -> 136 us
  blocking collectives: 51.7 us -> 0 us
  waiting for transfers between devices: 169 us -> 125 us
  matrix products: 43.1 us -> 36.5 us
    all_to_all x3 -> x0, waiting for transfers between devices: 150 us -> none  [the longest x1 52.5 us: on_device(): s2 = lax.all_to_all(s2, 'gx', 0, 0, tiled=True)]
    ppermute x0 -> x36, starting transfers between devices: none -> 134 us  [exchange(): got = lax.ppermute(piece, axis, [(s, (s + d) % n) for s in range(n)])]
    ppermute x0 -> x36, waiting for transfers between devices: none -> 106 us  [exchange(): got = lax.ppermute(piece, axis, [(s, (s + d) % n) for s in range(n)])]
    all_to_all x1 -> x0, blocking collectives: 51.7 us -> none  [on_device(): g2 = lax.all_to_all(g2, 'gy', 0, 0, tiled=True)]
    all_to_all x3 -> x0, starting transfers between devices: 25.7 us -> none  [the longest x1 12.7 us: on_device(): g1 = lax.all_to_all(g1, 'gx', 0, 0, tiled=True)]
    transpose x3 -> x0, local copies, waits for them, and re-layouts: 8.67 us -> none  [the longest x1 4.4 us: on_device(): s2 = jnp.einsum('jszxc,sjxrib->irbzc', s1, tx, precision=DFT)]
    unnamed x8 -> x41, local copies, waits for them, and re-layouts: 1.05 us -> 6.04 us
    sin x2 -> x0, other arithmetic: 4.25 us -> none  [on_device(): cx, sx = (jnp.cos(ang_x), jnp.sin(ang_x))]
  transfers between devices with their start and end apart: 4 -> 37, of which waited for: 4 -> 14; matrix products, arithmetic and copies ran while one was open for 4% -> 5% of each run, Pallas kernels for 0% -> 0%
where the time goes in v4:
time: 337 us; the launch traced here: 331 us
  starting transfers between devices  136 us (40%)
  waiting for transfers between devices  125 us (37%)
  matrix products  36.5 us (11%)
  other arithmetic  21 us (6%)
  local copies, waits for them, and re-layouts  11.2 us (3%)
    ppermute x36, starting transfers between devices, exchange(): got = lax.ppermute(piece, axis, [(s, (s + d) % n) for s in range(n)])  134 us
    ppermute x36, waiting for transfers between devices, exchange(): got = lax.ppermute(piece, axis, [(s, (s + d) % n) for s in range(n)])  106 us
    ppermute x1, waiting for transfers between devices, on_device(): recv = lax.ppermute(send[rows_k].astype(jnp.bfloat16), 'sta', pairs)  18.9 us
    dot_general x1, matrix products, on_device(): jnp.dot(coef, weights.reshape(own, rows * width), preferred_element_type=...  9.38 us
  transfers between devices with their start and end apart: 37, of which 14 were waited for; matrix products, arithmetic and copies ran while one was open for 5% of the time, Pallas kernels for 0%

profile of v4, /device:TPU:0, one launch (start us, length us, event | category | flops | bytes accessed | tf_op | source)
XLA Modules:
  0.0 331.4 jit_solution(16961983054236066271)
XLA Ops:
  5.1 9.4 %fusion = f32[2,16,64,512]{3,1,2,0:T(8,128)} fusion(bf16[2,16,64,1]{1,0,2,3:T(2,128)(2,1)S(1)} %fusion.119, bf16[8,8,64,512]{3,2,1,0:T(8,128)(2,1)} %bitcast.341), kind=kOutput, calls=%fused_computation.3 | convolution fusion | flops 134217728 | bytes 8392704 | tf_op jit(solution)/shard_map/dot_general | solution.py:85
  18.3 4.1 %fusion.95 = (f32[512,4,1,128]{3,0,2,1:T(8,128)S(1)}, f32[512,4,1,128]{3,0,2,1:T(8,128)S(1)}) fusion(s32[4,128]{1,0:T(4,128)S(1)} %iota_add_fusion.4), kind=kLoop, calls=%fused_computation.129 | loop fusion | flops 3932160 | bytes 2099200 | tf_op jit(solution)/shard_map/cos | solution.py:96
  22.4 18.9 %collective-permute-done = bf16[16,64,512]{2,0,1:T(8,128)(2,1)S(1)} collective-permute-done((bf16[16,64,512]{2,0,1:T(8,128)(2,1)S(1)}, bf16[16,64,512]{2,0,1:T(8,128)(2,1)S(1)}, u32[]{:S(2)}, u32[]{:S(2)}) %collective-permute-start) | collective-permute-done | bytes 1048608 | tf_op jit(solution)/shard_map/ppermute | solution.py:106
  43.2 4.3 %convolution_bitcast_fusion = f32[4,2,16,64,128]{4,3,2,1,0:T(8,128)S(1)} fusion(f32[512,4,1,128]{3,0,2,1:T(8,128)S(1)} %get-tuple-element.58, f32[512,4,1,128]{3,0,2,1:T(8,128)S(1)} %get-tuple-element.57, f32[16,64,512,1,1]{2,0,1,4,3:T(8,128)S(1)} %fusion.54), kind=kOutput, calls=%fused_computation.33 | convolution fusion | flops 3221749760 | bytes 8388608 | tf_op jit(solution)/shard_map/zxy,ydrc->drzxc/dot_general | solution.py:108
  59.2 15.4 %collective-permute-done.1 = f32[2,16,64,128]{3,2,1,0:T(8,128)S(1)} collective-permute-done((f32[2,16,64,128]{3,2,1,0:T(8,128)S(1)}, f32[2,16,64,128]{3,2,1,0:T(8,128)S(1)}, u32[]{:S(2)}, u32[]{:S(2)}) %collective-permute-start.1) | collective-permute-done | bytes 1048608 | tf_op jit(solution)/shard_map/ppermute | solution.py:44
  74.6 22.8 %collective-permute-done.2 = f32[2,16,64,128]{3,2,1,0:T(8,128)S(1)} collective-permute-done((f32[2,16,64,128]{3,2,1,0:T(8,128)S(1)}, f32[2,16,64,128]{3,2,1,0:T(8,128)S(1)}, u32[]{:S(2)}, u32[]{:S(2)}) %collective-permute-start.2) | collective-permute-done | bytes 1048608 | tf_op jit(solution)/shard_map/ppermute | solution.py:44
  97.4 3.7 %fusion.31 = f32[16,2,16,16,128]{4,2,3,0,1:T(8,128)S(1)} fusion(f32[1,2,16,64,128]{4,3,2,1,0:T(8,128)S(1)} %bitcast.344, f32[1,2,16,64,128]{4,3,2,1,0:T(8,128)S(1)} %bitcast.343, f32[1,2,16,64,128]{4,3,2,1,0:T(8,128)S(1)} %bitcast.342, f32[1,2,16,64,128]{4,3,2,1,0:T(8,128)S(1)} %get-tuple-element.41, f32[1,4,64,1,16,16]{2,5,0,1,4,3:T(8,128)S(1)} %get-tuple-element.50, ...), kind=kOutput, calls=%fused_computation.32 | convolution fusion | flops 3225157632 | bytes 9175040 | tf_op jit(solution)/shard_map/jszxc,sjxrib->irbzc/dot_general | solution.py:110
  110.5 3.6 %collective-permute-start.7 = (f32[2,16,16,128]{3,1,2,0:T(8,128)}, f32[2,16,16,128]{3,1,2,0:T(8,128)S(1)}, u32[]{:S(2)}, u32[]{:S(2)}) collective-permute-start(f32[2,16,16,128]{3,1,2,0:T(8,128)} %get-tuple-element.36), channel_id=1, source_target_pairs={{0,16},{4,20},{8,24},{12,28},{16,32},{20,36},{24,40},{28,44},{32,4... | collective-permute-start | bytes 786440 | tf_op jit(solution)/shard_map/ppermute | solution.py:44
  121.6 7.9 %collective-permute-start.10 = (f32[2,16,16,128]{3,1,2,0:T(8,128)}, f32[2,16,16,128]{3,1,2,0:T(8,128)S(1)}, u32[]{:S(2)}, u32[]{:S(2)}) collective-permute-start(f32[2,16,16,128]{3,1,2,0:T(8,128)} %get-tuple-element.33), channel_id=1, source_target_pairs={{0,28},{4,32},{8,36},{12,40},{16,44},{20,48},{24,52},{28,56},{32,6... | collective-permute-start | bytes 786440 | tf_op jit(solution)/shard_map/ppermute | solution.py:44
  129.5 4.4 %collective-permute-start.11 = (f32[2,16,16,128]{3,1,2,0:T(8,128)}, f32[2,16,16,128]{3,1,2,0:T(8,128)S(1)}, u32[]{:S(2)}, u32[]{:S(2)}) collective-permute-start(f32[2,16,16,128]{3,1,2,0:T(8,128)} %get-tuple-element.32), channel_id=1, source_target_pairs={{0,32},{4,36},{8,40},{12,44},{16,48},{20,52},{24,56},{28,60},{32,0... | collective-permute-start | bytes 786440 | tf_op jit(solution)/shard_map/ppermute | solution.py:44
  134.1 11.4 %collective-permute-start.13 = (f32[2,16,16,128]{3,1,2,0:T(8,128)S(1)}, f32[2,16,16,128]{3,1,2,0:T(8,128)S(1)}, u32[]{:S(2)}, u32[]{:S(2)}) collective-permute-start(f32[2,16,16,128]{3,1,2,0:T(8,128)S(1)} %get-tuple-element.30), channel_id=1, source_target_pairs={{0,40},{4,44},{8,48},{12,52},{16,56},{20,60},{24,0},{28,4},{32,8},... | collective-permute-start | bytes 786440 | tf_op jit(solution)/shard_map/ppermute | solution.py:44
  145.5 6.5 %collective-permute-start.14 = (f32[2,16,16,128]{3,1,2,0:T(8,128)S(1)}, f32[2,16,16,128]{3,1,2,0:T(8,128)S(1)}, u32[]{:S(2)}, u32[]{:S(2)}) collective-permute-start(f32[2,16,16,128]{3,1,2,0:T(8,128)S(1)} %get-tuple-element.29), channel_id=1, source_target_pairs={{0,44},{4,48},{8,52},{12,56},{16,60},{20,0},{24,4},{28,8},{32,12},... | collective-permute-start | bytes 786440 | tf_op jit(solution)/shard_map/ppermute | solution.py:44
  152.1 9.4 %collective-permute-start.15 = (f32[2,16,16,128]{3,1,2,0:T(8,128)S(1)}, f32[2,16,16,128]{3,1,2,0:T(8,128)S(1)}, u32[]{:S(2)}, u32[]{:S(2)}) collective-permute-start(f32[2,16,16,128]{3,1,2,0:T(8,128)S(1)} %get-tuple-element.28), channel_id=1, source_target_pairs={{0,48},{4,52},{8,56},{12,60},{16,0},{20,4},{24,8},{28,12},{32,16},... | collective-permute-start | bytes 786440 | tf_op jit(solution)/shard_map/ppermute | solution.py:44
  163.2 5.8 %collective-permute-start.17 = (f32[2,16,16,128]{3,1,2,0:T(8,128)S(1)}, f32[2,16,16,128]{3,1,2,0:T(8,128)S(1)}, u32[]{:S(2)}, u32[]{:S(2)}) collective-permute-start(f32[2,16,16,128]{3,1,2,0:T(8,128)S(1)} %get-tuple-element.40), channel_id=1, source_target_pairs={{0,56},{4,60},{8,0},{12,4},{16,8},{20,12},{24,16},{28,20},{32,24},... | collective-permute-start | bytes 786440 | tf_op jit(solution)/shard_map/ppermute | solution.py:44
  173.1 4.3 %collective-permute-done.16 = f32[2,16,16,128]{3,1,2,0:T(8,128)S(1)} collective-permute-done((f32[2,16,16,128]{3,1,2,0:T(8,128)S(1)}, f32[2,16,16,128]{3,1,2,0:T(8,128)S(1)}, u32[]{:S(2)}, u32[]{:S(2)}) %collective-permute-start.16) | collective-permute-done | bytes 262176 | tf_op jit(solution)/shard_map/ppermute | solution.py:44
  177.5 5.5 %collective-permute-done.17 = f32[2,16,16,128]{3,1,2,0:T(8,128)S(1)} collective-permute-done((f32[2,16,16,128]{3,1,2,0:T(8,128)S(1)}, f32[2,16,16,128]{3,1,2,0:T(8,128)S(1)}, u32[]{:S(2)}, u32[]{:S(2)}) %collective-permute-start.17) | collective-permute-done | bytes 262176 | tf_op jit(solution)/shard_map/ppermute | solution.py:44
  186.4 4.4 %fusion.25 = f32[2,256,16,128]{3,1,2,0:T(8,128)S(1)} fusion(f32[16,2,16,16,128]{4,2,3,1,0:T(8,128)S(1)} %bitcast_dynamic-update-slice_fusion.15, f32[1,16,16,1,256]{4,2,0,1,3:T(8,128)S(1)} %get-tuple-element.56, f32[1,16,16,1,256]{4,2,0,1,3:T(8,128)S(1)} %get-tuple-element.55, f32[1,16,16,1,256]{4,2,0,1,3:T(8,128)S(1)} %get-tuple-element.54), kind=kOutput, calls=%fused_computation.30 | convolution fusion | flops 3222011904 | bytes 9175040 | tf_op jit(solution)/shard_map/isbzc,sizra->rabc/dot_general | solution.py:112
  203.4 5.9 %collective-permute-start.23 = (f32[2,16,16,128]{3,1,2,0:T(8,128)S(1)}, f32[2,16,16,128]{3,1,2,0:T(8,128)S(1)}, u32[]{:S(2)}, u32[]{:S(2)}) collective-permute-start(f32[2,16,16,128]{3,1,2,0:T(8,128)S(1)} %get-tuple-element.20), channel_id=1, source_target_pairs={{0,20},{4,24},{8,28},{12,32},{16,36},{20,40},{24,44},{28,48},{32,5... | collective-permute-start | bytes 786440 | tf_op jit(solution)/shard_map/ppermute | solution.py:44
  209.3 7.1 %collective-permute-done.20 = f32[2,16,16,128]{3,1,2,0:T(8,128)S(1)} collective-permute-done((f32[2,16,16,128]{3,1,2,0:T(8,128)S(1)}, f32[2,16,16,128]{3,1,2,0:T(8,128)S(1)}, u32[]{:S(2)}, u32[]{:S(2)}) %collective-permute-start.20) | collective-permute-done | bytes 262176 | tf_op jit(solution)/shard_map/ppermute | solution.py:44
  220.4 4.7 %collective-permute-start.27 = (f32[2,16,16,128]{3,1,2,0:T(8,128)S(1)}, f32[2,16,16,128]{3,1,2,0:T(8,128)S(1)}, u32[]{:S(2)}, u32[]{:S(2)}) collective-permute-start(f32[2,16,16,128]{3,1,2,0:T(8,128)S(1)} %get-tuple-element.16), channel_id=1, source_target_pairs={{0,36},{4,40},{8,44},{12,48},{16,52},{20,56},{24,60},{28,0},{32,4}... | collective-permute-start | bytes 786440 | tf_op jit(solution)/shard_map/ppermute | solution.py:44
  225.1 9.0 %collective-permute-start.28 = (f32[2,16,16,128]{3,1,2,0:T(8,128)S(1)}, f32[2,16,16,128]{3,1,2,0:T(8,128)S(1)}, u32[]{:S(2)}, u32[]{:S(2)}) collective-permute-start(f32[2,16,16,128]{3,1,2,0:T(8,128)S(1)} %get-tuple-element.15), channel_id=1, source_target_pairs={{0,40},{4,44},{8,48},{12,52},{16,56},{20,60},{24,0},{28,4},{32,8},... | collective-permute-start | bytes 786440 | tf_op jit(solution)/shard_map/ppermute | solution.py:44
  234.2 7.1 %collective-permute-start.29 = (f32[2,16,16,128]{3,1,2,0:T(8,128)S(1)}, f32[2,16,16,128]{3,1,2,0:T(8,128)S(1)}, u32[]{:S(2)}, u32[]{:S(2)}) collective-permute-start(f32[2,16,16,128]{3,1,2,0:T(8,128)S(1)} %get-tuple-element.14), channel_id=1, source_target_pairs={{0,44},{4,48},{8,52},{12,56},{16,60},{20,0},{24,4},{28,8},{32,12},... | collective-permute-start | bytes 786440 | tf_op jit(solution)/shard_map/ppermute | solution.py:44
  241.3 6.5 %collective-permute-start.30 = (f32[2,16,16,128]{3,1,2,0:T(8,128)S(1)}, f32[2,16,16,128]{3,1,2,0:T(8,128)S(1)}, u32[]{:S(2)}, u32[]{:S(2)}) collective-permute-start(f32[2,16,16,128]{3,1,2,0:T(8,128)S(1)} %get-tuple-element.13), channel_id=1, source_target_pairs={{0,48},{4,52},{8,56},{12,60},{16,0},{20,4},{24,8},{28,12},{32,16},... | collective-permute-start | bytes 786440 | tf_op jit(solution)/shard_map/ppermute | solution.py:44
  247.9 5.2 %collective-permute-start.31 = (f32[2,16,16,128]{3,1,2,0:T(8,128)S(1)}, f32[2,16,16,128]{3,1,2,0:T(8,128)S(1)}, u32[]{:S(2)}, u32[]{:S(2)}) collective-permute-start(f32[2,16,16,128]{3,1,2,0:T(8,128)S(1)} %get-tuple-element.12), channel_id=1, source_target_pairs={{0,52},{4,56},{8,60},{12,0},{16,4},{20,8},{24,12},{28,16},{32,20},... | collective-permute-start | bytes 786440 | tf_op jit(solution)/shard_map/ppermute | solution.py:44
  253.2 6.0 %collective-permute-start.32 = (f32[2,16,16,128]{3,1,2,0:T(8,128)S(1)}, f32[2,16,16,128]{3,1,2,0:T(8,128)S(1)}, u32[]{:S(2)}, u32[]{:S(2)}) collective-permute-start(f32[2,16,16,128]{3,1,2,0:T(8,128)S(1)} %get-tuple-element.25), channel_id=1, source_target_pairs={{0,56},{4,60},{8,0},{12,4},{16,8},{20,12},{24,16},{28,20},{32,24},... | collective-permute-start | bytes 786440 | tf_op jit(solution)/shard_map/ppermute | solution.py:44
  259.2 5.4 %collective-permute-start.33 = (f32[2,16,16,128]{3,1,2,0:T(8,128)S(1)}, f32[2,16,16,128]{3,1,2,0:T(8,128)S(1)}, u32[]{:S(2)}, u32[]{:S(2)}) collective-permute-start(f32[2,16,16,128]{3,1,2,0:T(8,128)S(1)} %get-tuple-element.11), channel_id=1, source_target_pairs={{0,60},{4,0},{8,4},{12,8},{16,12},{20,16},{24,20},{28,24},{32,28},... | collective-permute-start | bytes 786440 | tf_op jit(solution)/shard_map/ppermute | solution.py:44
  268.7 5.7 %fusion.28 = f32[4,2,16,64,128]{4,3,2,0,1:T(8,128)S(1)} fusion(f32[16,2,16,16,128,1,1]{4,2,3,1,0,6,5:T(8,128)S(1)} %bitcast.340, f32[1,16,16,1,4,64]{5,1,0,2,4,3:T(8,128)S(1)} %get-tuple-element.47, f32[1,16,16,1,4,64]{5,1,0,2,4,3:T(8,128)S(1)} %get-tuple-element.46, f32[1,16,16,1,4,64]{5,1,0,2,4,3:T(8,128)S(1)} %get-tuple-element.45), kind=kOutput, calls=%fused_computation.31 | convolution fusion | flops 3222011904 | bytes 9175040 | tf_op jit(solution)/shard_map/iszbc,sibrjx->jrzxc/dot_general | solution.py:133
  276.0 4.2 %collective-permute-start.35 = (f32[2,16,64,128]{3,2,1,0:T(8,128)S(1)}, f32[2,16,64,128]{3,2,1,0:T(8,128)S(1)}, u32[]{:S(2)}, u32[]{:S(2)}) collective-permute-start(f32[2,16,64,128]{3,2,1,0:T(8,128)S(1)} %get-tuple-element.10), channel_id=1, source_target_pairs={{0,2},{1,3},{2,0},{3,1},{4,6},{5,7},{6,4},{7,5},{8,10},{9,11},{10,... | collective-permute-start | bytes 3145736 | tf_op jit(solution)/shard_map/ppermute | solution.py:44
  280.6 4.2 %fusion.94 = (f32[4,1,128,512]{3,2,1,0:T(8,128)S(1)}, f32[4,1,128,512]{3,2,1,0:T(8,128)S(1)}) fusion(s32[4,128]{1,0:T(4,128)S(1)} %iota_add_fusion.3), kind=kLoop, calls=%fused_computation.128 | loop fusion | flops 3932160 | bytes 2099200 | tf_op jit(solution)/shard_map/cos | solution.py:126
  284.8 17.6 %collective-permute-done.34 = f32[2,16,64,128]{3,2,1,0:T(8,128)S(1)} collective-permute-done((f32[2,16,64,128]{3,2,1,0:T(8,128)S(1)}, f32[2,16,64,128]{3,2,1,0:T(8,128)S(1)}, u32[]{:S(2)}, u32[]{:S(2)}) %collective-permute-start.34) | collective-permute-done | bytes 1048608 | tf_op jit(solution)/shard_map/ppermute | solution.py:44
  302.4 23.6 %collective-permute-done.35 = f32[2,16,64,128]{3,2,1,0:T(8,128)S(1)} collective-permute-done((f32[2,16,64,128]{3,2,1,0:T(8,128)S(1)}, f32[2,16,64,128]{3,2,1,0:T(8,128)S(1)}, u32[]{:S(2)}, u32[]{:S(2)}) %collective-permute-start.35) | collective-permute-done | bytes 1048608 | tf_op jit(solution)/shard_map/ppermute | solution.py:44
  326.1 4.8 %fusion.55 = f32[1,16,64,512]{3,2,1,0:T(8,128)} fusion(f32[4,1,128,512]{3,2,1,0:T(8,128)S(1)} %get-tuple-element.60, f32[4,1,128,512]{3,2,1,0:T(8,128)S(1)} %get-tuple-element.59, f32[1,2,16,64,128]{4,3,2,1,0:T(8,128)S(1)} %bitcast.347, f32[1,2,16,64,128]{4,3,2,1,0:T(8,128)S(1)} %bitcast.346, f32[1,2,16,64,128]{4,3,2,1,0:T(8,128)S(1)} %bitcast.345, ...), kind=kOutput, calls=%fused_computation.66 | convolution fusion | flops 3225419776 | bytes 8388608 | tf_op jit(solution)/shard_map/jrzxc,jrcy->zxy/dot_general | solution.py:135
  (123 shorter events, 71.4 us)
Async XLA Ops:
  16.3 25.0 %collective-permute-start = (bf16[16,64,512]{2,0,1:T(8,128)(2,1)S(1)}, bf16[16,64,512]{2,0,1:T(8,128)(2,1)S(1)}, u32[]{:S(2)}, u32[]{:S(2)}) collective-permute-start(bf16[16,64,512]{2,0,1:T(8,128)(2,1)S(1)} %fusion.66), channel_id=1, source_target_pairs={{0,64},{64,0},{1,65},{65,1},{2,66},{66,2},{3,67},{67,3},{4,68},{68... | collective-permute-start | bytes 3145736 | tf_op jit(solution)/shard_map/ppermute | solution.py:106
  48.1 26.5 %collective-permute-start.1 = (f32[2,16,64,128]{3,2,1,0:T(8,128)S(1)}, f32[2,16,64,128]{3,2,1,0:T(8,128)S(1)}, u32[]{:S(2)}, u32[]{:S(2)}) collective-permute-start(f32[2,16,64,128]{3,2,1,0:T(8,128)S(1)} %get-tuple-element.44), channel_id=1, source_target_pairs={{0,1},{1,2},{2,3},{3,0},{4,5},{5,6},{6,7},{7,4},{8,9},{9,10},{10,1... | collective-permute-start | bytes 3145736 | tf_op jit(solution)/shard_map/ppermute | solution.py:44
  50.0 47.4 %collective-permute-start.2 = (f32[2,16,64,128]{3,2,1,0:T(8,128)S(1)}, f32[2,16,64,128]{3,2,1,0:T(8,128)S(1)}, u32[]{:S(2)}, u32[]{:S(2)}) collective-permute-start(f32[2,16,64,128]{3,2,1,0:T(8,128)S(1)} %get-tuple-element.43), channel_id=1, source_target_pairs={{0,2},{1,3},{2,0},{3,1},{4,6},{5,7},{6,4},{7,5},{8,10},{9,11},{10,... | collective-permute-start | bytes 3145736 | tf_op jit(solution)/shard_map/ppermute | solution.py:44
  52.9 44.5 %collective-permute-start.3 = (f32[2,16,64,128]{3,2,1,0:T(8,128)S(1)}, f32[2,16,64,128]{3,2,1,0:T(8,128)S(1)}, u32[]{:S(2)}, u32[]{:S(2)}) collective-permute-start(f32[2,16,64,128]{3,2,1,0:T(8,128)S(1)} %get-tuple-element.42), channel_id=1, source_target_pairs={{0,3},{1,0},{2,1},{3,2},{4,7},{5,4},{6,5},{7,6},{8,11},{9,8},{10,9... | collective-permute-start | bytes 3145736 | tf_op jit(solution)/shard_map/ppermute | solution.py:44
  104.6 17.1 %collective-permute-start.5 = (f32[2,16,16,128]{3,1,2,0:T(8,128)}, f32[2,16,16,128]{3,1,2,0:T(8,128)S(1)}, u32[]{:S(2)}, u32[]{:S(2)}) collective-permute-start(f32[2,16,16,128]{3,1,2,0:T(8,128)} %get-tuple-element.38), channel_id=1, source_target_pairs={{0,8},{4,12},{8,16},{12,20},{16,24},{20,28},{24,32},{28,36},{32,40... | collective-permute-start | bytes 786440 | tf_op jit(solution)/shard_map/ppermute | solution.py:44
  107.4 22.1 %collective-permute-start.6 = (f32[2,16,16,128]{3,1,2,0:T(8,128)}, f32[2,16,16,128]{3,1,2,0:T(8,128)S(1)}, u32[]{:S(2)}, u32[]{:S(2)}) collective-permute-start(f32[2,16,16,128]{3,1,2,0:T(8,128)} %get-tuple-element.37), channel_id=1, source_target_pairs={{0,12},{4,16},{8,20},{12,24},{16,28},{20,32},{24,36},{28,40},{32,4... | collective-permute-start | bytes 786440 | tf_op jit(solution)/shard_map/ppermute | solution.py:44
  110.5 23.5 %collective-permute-start.7 = (f32[2,16,16,128]{3,1,2,0:T(8,128)}, f32[2,16,16,128]{3,1,2,0:T(8,128)S(1)}, u32[]{:S(2)}, u32[]{:S(2)}) collective-permute-start(f32[2,16,16,128]{3,1,2,0:T(8,128)} %get-tuple-element.36), channel_id=1, source_target_pairs={{0,16},{4,20},{8,24},{12,28},{16,32},{20,36},{24,40},{28,44},{32,4... | collective-permute-start | bytes 786440 | tf_op jit(solution)/shard_map/ppermute | solution.py:44
  114.1 20.0 %collective-permute-start.8 = (f32[2,16,16,128]{3,1,2,0:T(8,128)}, f32[2,16,16,128]{3,1,2,0:T(8,128)S(1)}, u32[]{:S(2)}, u32[]{:S(2)}) collective-permute-start(f32[2,16,16,128]{3,1,2,0:T(8,128)} %get-tuple-element.35), channel_id=1, source_target_pairs={{0,20},{4,24},{8,28},{12,32},{16,36},{20,40},{24,44},{28,48},{32,5... | collective-permute-start | bytes 786440 | tf_op jit(solution)/shard_map/ppermute | solution.py:44
  116.5 29.0 %collective-permute-start.9 = (f32[2,16,16,128]{3,1,2,0:T(8,128)}, f32[2,16,16,128]{3,1,2,0:T(8,128)S(1)}, u32[]{:S(2)}, u32[]{:S(2)}) collective-permute-start(f32[2,16,16,128]{3,1,2,0:T(8,128)} %get-tuple-element.34), channel_id=1, source_target_pairs={{0,24},{4,28},{8,32},{12,36},{16,40},{20,44},{24,48},{28,52},{32,5... | collective-permute-start | bytes 786440 | tf_op jit(solution)/shard_map/ppermute | solution.py:44
  121.6 30.5 %collective-permute-start.10 = (f32[2,16,16,128]{3,1,2,0:T(8,128)}, f32[2,16,16,128]{3,1,2,0:T(8,128)S(1)}, u32[]{:S(2)}, u32[]{:S(2)}) collective-permute-start(f32[2,16,16,128]{3,1,2,0:T(8,128)} %get-tuple-element.33), channel_id=1, source_target_pairs={{0,28},{4,32},{8,36},{12,40},{16,44},{20,48},{24,52},{28,56},{32,6... | collective-permute-start | bytes 786440 | tf_op jit(solution)/shard_map/ppermute | solution.py:44
  129.5 32.0 %collective-permute-start.11 = (f32[2,16,16,128]{3,1,2,0:T(8,128)}, f32[2,16,16,128]{3,1,2,0:T(8,128)S(1)}, u32[]{:S(2)}, u32[]{:S(2)}) collective-permute-start(f32[2,16,16,128]{3,1,2,0:T(8,128)} %get-tuple-element.32), channel_id=1, source_target_pairs={{0,32},{4,36},{8,40},{12,44},{16,48},{20,52},{24,56},{28,60},{32,0... | collective-permute-start | bytes 786440 | tf_op jit(solution)/shard_map/ppermute | solution.py:44
  134.0 29.3 %collective-permute-start.12 = (f32[2,16,16,128]{3,1,2,0:T(8,128)S(1)}, f32[2,16,16,128]{3,1,2,0:T(8,128)S(1)}, u32[]{:S(2)}, u32[]{:S(2)}) collective-permute-start(f32[2,16,16,128]{3,1,2,0:T(8,128)S(1)} %get-tuple-element.31), channel_id=1, source_target_pairs={{0,36},{4,40},{8,44},{12,48},{16,52},{20,56},{24,60},{28,0},{32,4}... | collective-permute-start | bytes 786440 | tf_op jit(solution)/shard_map/ppermute | solution.py:44
  134.1 34.9 %collective-permute-start.13 = (f32[2,16,16,128]{3,1,2,0:T(8,128)S(1)}, f32[2,16,16,128]{3,1,2,0:T(8,128)S(1)}, u32[]{:S(2)}, u32[]{:S(2)}) collective-permute-start(f32[2,16,16,128]{3,1,2,0:T(8,128)S(1)} %get-tuple-element.30), channel_id=1, source_target_pairs={{0,40},{4,44},{8,48},{12,52},{16,56},{20,60},{24,0},{28,4},{32,8},... | collective-permute-start | bytes 786440 | tf_op jit(solution)/shard_map/ppermute | solution.py:44
  145.5 27.1 %collective-permute-start.14 = (f32[2,16,16,128]{3,1,2,0:T(8,128)S(1)}, f32[2,16,16,128]{3,1,2,0:T(8,128)S(1)}, u32[]{:S(2)}, u32[]{:S(2)}) collective-permute-start(f32[2,16,16,128]{3,1,2,0:T(8,128)S(1)} %get-tuple-element.29), channel_id=1, source_target_pairs={{0,44},{4,48},{8,52},{12,56},{16,60},{20,0},{24,4},{28,8},{32,12},... | collective-permute-start | bytes 786440 | tf_op jit(solution)/shard_map/ppermute | solution.py:44
  152.1 21.0 %collective-permute-start.15 = (f32[2,16,16,128]{3,1,2,0:T(8,128)S(1)}, f32[2,16,16,128]{3,1,2,0:T(8,128)S(1)}, u32[]{:S(2)}, u32[]{:S(2)}) collective-permute-start(f32[2,16,16,128]{3,1,2,0:T(8,128)S(1)} %get-tuple-element.28), channel_id=1, source_target_pairs={{0,48},{4,52},{8,56},{12,60},{16,0},{20,4},{24,8},{28,12},{32,16},... | collective-permute-start | bytes 786440 | tf_op jit(solution)/shard_map/ppermute | solution.py:44
  163.2 19.7 %collective-permute-start.17 = (f32[2,16,16,128]{3,1,2,0:T(8,128)S(1)}, f32[2,16,16,128]{3,1,2,0:T(8,128)S(1)}, u32[]{:S(2)}, u32[]{:S(2)}) collective-permute-start(f32[2,16,16,128]{3,1,2,0:T(8,128)S(1)} %get-tuple-element.40), channel_id=1, source_target_pairs={{0,56},{4,60},{8,0},{12,4},{16,8},{20,12},{24,16},{28,20},{32,24},... | collective-permute-start | bytes 786440 | tf_op jit(solution)/shard_map/ppermute | solution.py:44
  169.0 17.3 %collective-permute-start.18 = (f32[2,16,16,128]{3,1,2,0:T(8,128)S(1)}, f32[2,16,16,128]{3,1,2,0:T(8,128)S(1)}, u32[]{:S(2)}, u32[]{:S(2)}) collective-permute-start(f32[2,16,16,128]{3,1,2,0:T(8,128)S(1)} %get-tuple-element.26), channel_id=1, source_target_pairs={{0,60},{4,0},{8,4},{12,8},{16,12},{20,16},{24,20},{28,24},{32,28},... | collective-permute-start | bytes 786440 | tf_op jit(solution)/shard_map/ppermute | solution.py:44
  198.7 17.8 %collective-permute-start.20 = (f32[2,16,16,128]{3,1,2,0:T(8,128)S(1)}, f32[2,16,16,128]{3,1,2,0:T(8,128)S(1)}, u32[]{:S(2)}, u32[]{:S(2)}) collective-permute-start(f32[2,16,16,128]{3,1,2,0:T(8,128)S(1)} %get-tuple-element.23), channel_id=1, source_target_pairs={{0,8},{4,12},{8,16},{12,20},{16,24},{20,28},{24,32},{28,36},{32,40... | collective-permute-start | bytes 786440 | tf_op jit(solution)/shard_map/ppermute | solution.py:44
  198.8 17.7 %collective-permute-start.21 = (f32[2,16,16,128]{3,1,2,0:T(8,128)S(1)}, f32[2,16,16,128]{3,1,2,0:T(8,128)S(1)}, u32[]{:S(2)}, u32[]{:S(2)}) collective-permute-start(f32[2,16,16,128]{3,1,2,0:T(8,128)S(1)} %get-tuple-element.22), channel_id=1, source_target_pairs={{0,12},{4,16},{8,20},{12,24},{16,28},{20,32},{24,36},{28,40},{32,4... | collective-permute-start | bytes 786440 | tf_op jit(solution)/shard_map/ppermute | solution.py:44
  200.1 20.3 %collective-permute-start.22 = (f32[2,16,16,128]{3,1,2,0:T(8,128)S(1)}, f32[2,16,16,128]{3,1,2,0:T(8,128)S(1)}, u32[]{:S(2)}, u32[]{:S(2)}) collective-permute-start(f32[2,16,16,128]{3,1,2,0:T(8,128)S(1)} %get-tuple-element.21), channel_id=1, source_target_pairs={{0,16},{4,20},{8,24},{12,28},{16,32},{20,36},{24,40},{28,44},{32,4... | collective-permute-start | bytes 786440 | tf_op jit(solution)/shard_map/ppermute | solution.py:44
  203.4 21.7 %collective-permute-start.23 = (f32[2,16,16,128]{3,1,2,0:T(8,128)S(1)}, f32[2,16,16,128]{3,1,2,0:T(8,128)S(1)}, u32[]{:S(2)}, u32[]{:S(2)}) collective-permute-start(f32[2,16,16,128]{3,1,2,0:T(8,128)S(1)} %get-tuple-element.20), channel_id=1, source_target_pairs={{0,20},{4,24},{8,28},{12,32},{16,36},{20,40},{24,44},{28,48},{32,5... | collective-permute-start | bytes 786440 | tf_op jit(solution)/shard_map/ppermute | solution.py:44
  209.3 24.8 %collective-permute-start.24 = (f32[2,16,16,128]{3,1,2,0:T(8,128)S(1)}, f32[2,16,16,128]{3,1,2,0:T(8,128)S(1)}, u32[]{:S(2)}, u32[]{:S(2)}) collective-permute-start(f32[2,16,16,128]{3,1,2,0:T(8,128)S(1)} %get-tuple-element.19), channel_id=1, source_target_pairs={{0,24},{4,28},{8,32},{12,36},{16,40},{20,44},{24,48},{28,52},{32,5... | collective-permute-start | bytes 786440 | tf_op jit(solution)/shard_map/ppermute | solution.py:44
  216.5 24.9 %collective-permute-start.25 = (f32[2,16,16,128]{3,1,2,0:T(8,128)S(1)}, f32[2,16,16,128]{3,1,2,0:T(8,128)S(1)}, u32[]{:S(2)}, u32[]{:S(2)}) collective-permute-start(f32[2,16,16,128]{3,1,2,0:T(8,128)S(1)} %get-tuple-element.18), channel_id=1, source_target_pairs={{0,28},{4,32},{8,36},{12,40},{16,44},{20,48},{24,52},{28,56},{32,6... | collective-permute-start | bytes 786440 | tf_op jit(solution)/shard_map/ppermute | solution.py:44
  216.5 31.4 %collective-permute-start.26 = (f32[2,16,16,128]{3,1,2,0:T(8,128)S(1)}, f32[2,16,16,128]{3,1,2,0:T(8,128)S(1)}, u32[]{:S(2)}, u32[]{:S(2)}) collective-permute-start(f32[2,16,16,128]{3,1,2,0:T(8,128)S(1)} %get-tuple-element.17), channel_id=1, source_target_pairs={{0,32},{4,36},{8,40},{12,44},{16,48},{20,52},{24,56},{28,60},{32,0... | collective-permute-start | bytes 786440 | tf_op jit(solution)/shard_map/ppermute | solution.py:44
  220.4 32.8 %collective-permute-start.27 = (f32[2,16,16,128]{3,1,2,0:T(8,128)S(1)}, f32[2,16,16,128]{3,1,2,0:T(8,128)S(1)}, u32[]{:S(2)}, u32[]{:S(2)}) collective-permute-start(f32[2,16,16,128]{3,1,2,0:T(8,128)S(1)} %get-tuple-element.16), channel_id=1, source_target_pairs={{0,36},{4,40},{8,44},{12,48},{16,52},{20,56},{24,60},{28,0},{32,4}... | collective-permute-start | bytes 786440 | tf_op jit(solution)/shard_map/ppermute | solution.py:44
  225.1 34.1 %collective-permute-start.28 = (f32[2,16,16,128]{3,1,2,0:T(8,128)S(1)}, f32[2,16,16,128]{3,1,2,0:T(8,128)S(1)}, u32[]{:S(2)}, u32[]{:S(2)}) collective-permute-start(f32[2,16,16,128]{3,1,2,0:T(8,128)S(1)} %get-tuple-element.15), channel_id=1, source_target_pairs={{0,40},{4,44},{8,48},{12,52},{16,56},{20,60},{24,0},{28,4},{32,8},... | collective-permute-start | bytes 786440 | tf_op jit(solution)/shard_map/ppermute | solution.py:44
  234.2 30.5 %collective-permute-start.29 = (f32[2,16,16,128]{3,1,2,0:T(8,128)S(1)}, f32[2,16,16,128]{3,1,2,0:T(8,128)S(1)}, u32[]{:S(2)}, u32[]{:S(2)}) collective-permute-start(f32[2,16,16,128]{3,1,2,0:T(8,128)S(1)} %get-tuple-element.14), channel_id=1, source_target_pairs={{0,44},{4,48},{8,52},{12,56},{16,60},{20,0},{24,4},{28,8},{32,12},... | collective-permute-start | bytes 786440 | tf_op jit(solution)/shard_map/ppermute | solution.py:44
  241.3 23.4 %collective-permute-start.30 = (f32[2,16,16,128]{3,1,2,0:T(8,128)S(1)}, f32[2,16,16,128]{3,1,2,0:T(8,128)S(1)}, u32[]{:S(2)}, u32[]{:S(2)}) collective-permute-start(f32[2,16,16,128]{3,1,2,0:T(8,128)S(1)} %get-tuple-element.13), channel_id=1, source_target_pairs={{0,48},{4,52},{8,56},{12,60},{16,0},{20,4},{24,8},{28,12},{32,16},... | collective-permute-start | bytes 786440 | tf_op jit(solution)/shard_map/ppermute | solution.py:44
  247.9 16.9 %collective-permute-start.31 = (f32[2,16,16,128]{3,1,2,0:T(8,128)S(1)}, f32[2,16,16,128]{3,1,2,0:T(8,128)S(1)}, u32[]{:S(2)}, u32[]{:S(2)}) collective-permute-start(f32[2,16,16,128]{3,1,2,0:T(8,128)S(1)} %get-tuple-element.12), channel_id=1, source_target_pairs={{0,52},{4,56},{8,60},{12,0},{16,4},{20,8},{24,12},{28,16},{32,20},... | collective-permute-start | bytes 786440 | tf_op jit(solution)/shard_map/ppermute | solution.py:44
  274.9 27.5 %collective-permute-start.34 = (f32[2,16,64,128]{3,2,1,0:T(8,128)S(1)}, f32[2,16,64,128]{3,2,1,0:T(8,128)S(1)}, u32[]{:S(2)}, u32[]{:S(2)}) collective-permute-start(f32[2,16,64,128]{3,2,1,0:T(8,128)S(1)} %get-tuple-element.8), channel_id=1, source_target_pairs={{0,1},{1,2},{2,3},{3,0},{4,5},{5,6},{6,7},{7,4},{8,9},{9,10},{10,1... | collective-permute-start | bytes 3145736 | tf_op jit(solution)/shard_map/ppermute | solution.py:44
  276.0 50.1 %collective-permute-start.35 = (f32[2,16,64,128]{3,2,1,0:T(8,128)S(1)}, f32[2,16,64,128]{3,2,1,0:T(8,128)S(1)}, u32[]{:S(2)}, u32[]{:S(2)}) collective-permute-start(f32[2,16,64,128]{3,2,1,0:T(8,128)S(1)} %get-tuple-element.10), channel_id=1, source_target_pairs={{0,2},{1,3},{2,0},{3,1},{4,6},{5,7},{6,4},{7,5},{8,10},{9,11},{10,... | collective-permute-start | bytes 3145736 | tf_op jit(solution)/shard_map/ppermute | solution.py:44
  280.3 45.8 %collective-permute-start.36 = (f32[2,16,64,128]{3,2,1,0:T(8,128)S(1)}, f32[2,16,64,128]{3,2,1,0:T(8,128)S(1)}, u32[]{:S(2)}, u32[]{:S(2)}) collective-permute-start(f32[2,16,64,128]{3,2,1,0:T(8,128)S(1)} %get-tuple-element.9), channel_id=1, source_target_pairs={{0,3},{1,0},{2,1},{3,2},{4,7},{5,4},{6,5},{7,6},{8,11},{9,8},{10,9... | collective-permute-start | bytes 3145736 | tf_op jit(solution)/shard_map/ppermute | solution.py:44
  (10 other events, 79.8 us)

commit v5 on v3

--- a/solution.py
+++ b/solution.py
@@ -81,8 +81,8 @@
     s3 = None
     for k in range(CHUNKS):
         rows_k = slice(k * zc, (k + 1) * zc)
-        recv = lax.ppermute(send[rows_k].astype(jnp.bfloat16), "sta", pairs)
-        stack = keep[rows_k] + recv.astype(jnp.float32)
+        recv = lax.ppermute(send[rows_k], "sta", pairs)
+        stack = keep[rows_k] + recv
         s1 = jnp.einsum("zxy,yjrc->jrzxc", stack, ty, precision=DFT)
         s1 = lax.all_to_all(s1, "gy", 0, 0, tiled=True)
         s2 = jnp.einsum("jszxc,sjxrib->irbzc", s1, tx, precision=DFT)

time: 292 us -> 313 us (1.072)
  waiting for transfers between devices: 145 us -> 167 us
    ppermute x1, waiting for transfers between devices: 19 us -> 41.5 us  [on_device(): recv = lax.ppermute(send[rows_k], 'sta', pairs)]
    dynamic_slice x0 -> x2, local copies, waits for them, and re-layouts: none -> 3.89 us  [the longest x1 2.67 us: on_device(): keep = lax.dynamic_index_in_dim(partial, k_sta, 0, keepdims=False)]
where the time goes in v5:
time: 313 us
  waiting for transfers between devices  167 us (53%)
  blocking collectives  51.5 us (16%)
  matrix products  39.5 us (13%)
  starting transfers between devices  27.3 us (9%)
  other arithmetic  15.4 us (5%)
  local copies, waits for them, and re-layouts  11.6 us (4%)
    all_to_all x1, waiting for transfers between devices, on_device(): s2 = lax.all_to_all(s2, 'gx', 0, 0, tiled=True)  53.2 us
    all_to_all x1, blocking collectives, on_device(): g2 = lax.all_to_all(g2, 'gy', 0, 0, tiled=True)  51.5 us
    all_to_all x1, waiting for transfers between devices, on_device(): s1 = lax.all_to_all(s1, 'gy', 0, 0, tiled=True)  46.3 us
    ppermute x1, waiting for transfers between devices, on_device(): recv = lax.ppermute(send[rows_k], 'sta', pairs)  41.5 us
    all_to_all x1, waiting for transfers between devices, on_device(): g1 = lax.all_to_all(g1.astype(jnp.bfloat16), 'gx', 0, 0, tiled=True)  26.2 us
    all_to_all x1, starting transfers between devices, on_device(): g1 = lax.all_to_all(g1.astype(jnp.bfloat16), 'gx', 0, 0, tiled=True)  12.7 us
    dot_general x1, matrix products, on_device(): jnp.dot(coef, weights.reshape(own, rows * width), preferred_element_type=...  9.39 us
    all_to_all x1, starting transfers between devices, on_device(): s2 = lax.all_to_all(s2, 'gx', 0, 0, tiled=True)  7.99 us
  transfers between devices with their start and end apart: 4, of which 4 were waited for; matrix products, arithmetic and copies ran while one was open for 4% of the time, Pallas kernels for 0%

profile of v5, /device:TPU:0, one launch (start us, length us, event | category | flops | bytes accessed | tf_op | source)
XLA Modules:
  0.0 312.9 jit_solution(16248839614858788)
XLA Ops:
  0.0 1.0 copy-done
  1.1 0.8 constant_dynamic-slice_fusion.3
  2.0 0.8 convert_reduce_fusion
  2.7 0.8 convolution_bitcast_fusion.2
  3.6 1.4 select_reduce_fusion
  5.1 9.4 %fusion = f32[2,16,64,512]{3,1,2,0:T(8,128)} fusion(bf16[2,16,64,1]{1,0,2,3:T(2,128)(2,1)S(1)} %fusion.84, bf16[8,8,64,512]{3,2,1,0:T(8,128)(2,1)} %bitcast.133), kind=kOutput, calls=%fused_computation.3 | convolution fusion | flops 134217728 | bytes 8392704 | tf_op jit(solution)/shard_map/dot_general | solution.py:59
  14.5 2.7 constant_dynamic-slice_fusion.1
  17.2 1.2 copy.152
  18.4 1.8 collective-permute-start
  20.3 4.1 %fusion.57 = (f32[512,4,1,128]{3,0,2,1:T(8,128)S(1)}, f32[512,4,1,128]{3,0,2,1:T(8,128)S(1)}) fusion(s32[4,128]{1,0:T(4,128)S(1)} %multiply_add_fusion.1), kind=kLoop, calls=%fused_computation.85 | loop fusion | flops 3932160 | bytes 2099200 | tf_op jit(solution)/shard_map/cos | solution.py:69
  24.4 41.5 %collective-permute-done = f32[16,64,512]{2,1,0:T(8,128)S(1)} collective-permute-done((f32[16,64,512]{2,1,0:T(8,128)S(1)}, f32[16,64,512]{2,1,0:T(8,128)S(1)}, u32[]{:S(2)}, u32[]{:S(2)}) %collective-permute-start) | collective-permute-done | bytes 2097184 | tf_op jit(solution)/shard_map/ppermute | solution.py:84
  65.9 5.8 %convolution_bitcast_fusion.1 = f32[4,2,16,64,128]{4,3,2,1,0:T(8,128)} fusion(f32[16,64,512]{2,1,0:T(8,128)S(1)} %collective-permute-done, f32[1,16,64,512]{3,1,2,0:T(8,128)S(1)} %get-tuple-element.7, f32[512,4,1,128]{3,0,2,1:T(8,128)S(1)} %get-tuple-element.22, f32[512,4,1,128]{3,0,2,1:T(8,128)S(1)} %get-tuple-element.21), kind=kOutput, calls=%fused_computation.18 | convolution fusion | flops 3222274048 | bytes 10485760 | tf_op jit(solution)/shard_map/zxy,yjrc->jrzxc/dot_general | solution.py:86
  71.7 4.8 %all-to-all-start = ((f32[4,2,16,64,128]{4,3,2,1,0:T(8,128)}), f32[4,2,16,64,128]{4,3,2,1,0:T(8,128)}, u32[]{:S(2)}, u32[]{:S(2)}) async-start(f32[4,2,16,64,128]{4,3,2,1,0:T(8,128)} %convolution_bitcast_fusion.1), calls=%async_computation | async-start | bytes 8388608 | tf_op jit(solution)/shard_map/all_to_all | solution.py:87
  76.6 2.1 fusion.76
  78.7 46.3 %all-to-all-done = f32[4,2,16,64,128]{4,3,2,1,0:T(8,128)} async-done(((f32[4,2,16,64,128]{4,3,2,1,0:T(8,128)}), f32[4,2,16,64,128]{4,3,2,1,0:T(8,128)}, u32[]{:S(2)}, u32[]{:S(2)}) %all-to-all-start) | async-done | bytes 4194336 | tf_op jit(solution)/shard_map/all_to_all | solution.py:87
  125.0 5.5 %fusion.10 = f32[16,2,16,16,128]{4,2,3,0,1:T(8,128)S(1)} fusion(f32[4,2,16,64,128]{4,3,2,1,0:T(8,128)} %all-to-all-done, f32[1,4,64,1,16,16]{2,5,4,3,1,0:T(8,128)S(1)} %get-tuple-element.11, f32[1,4,64,1,16,16]{2,5,4,3,1,0:T(8,128)S(1)} %get-tuple-element.10, f32[1,4,64,1,16,16]{2,5,4,3,1,0:T(8,128)S(1)} %get-tuple-element.9), kind=kOutput, calls=%fused_computation.15 | convolution fusion | flops 3222011904 | bytes 9175040 | tf_op jit(solution)/shard_map/jszxc,sjxrib->irbzc/dot_general | solution.py:88
  130.5 3.3 %copy.74 = f32[16,2,16,16,128]{4,3,1,2,0:T(8,128)} copy(f32[16,2,16,16,128]{4,2,3,0,1:T(8,128)S(1)} %fusion.10) | data formatting | bytes 8388608 | tf_op jit(solution)/shard_map/jszxc,sjxrib->irbzc/transpose | solution.py:88
  133.8 8.0 %all-to-all-start.1 = ((f32[16,2,16,16,128]{4,3,1,2,0:T(8,128)}), f32[16,2,16,16,128]{4,3,1,2,0:T(8,128)}, u32[]{:S(2)}, u32[]{:S(2)}) async-start(f32[16,2,16,16,128]{4,3,1,2,0:T(8,128)} %copy.74), calls=%async_computation.1 | async-start | bytes 8388608 | tf_op jit(solution)/shard_map/all_to_all | solution.py:89
  141.8 1.1 fusion.82
  142.9 1.1 fusion.79
  144.1 53.2 %all-to-all-done.1 = f32[16,2,16,16,128]{4,3,1,2,0:T(8,128)} async-done(((f32[16,2,16,16,128]{4,3,1,2,0:T(8,128)}), f32[16,2,16,16,128]{4,3,1,2,0:T(8,128)}, u32[]{:S(2)}, u32[]{:S(2)}) %all-to-all-start.1) | async-done | bytes 4194336 | tf_op jit(solution)/shard_map/all_to_all | solution.py:89
  197.3 5.6 %fusion.13 = f32[2,256,16,128]{3,1,2,0:T(8,128)S(1)} fusion(f32[16,2,16,16,128]{4,3,1,2,0:T(8,128)} %all-to-all-done.1, f32[1,16,16,1,256]{4,2,0,1,3:T(8,128)S(1)} %get-tuple-element.20, f32[1,16,16,1,256]{4,2,0,1,3:T(8,128)S(1)} %get-tuple-element.19, f32[1,16,16,1,256]{4,2,0,1,3:T(8,128)S(1)} %get-tuple-element.18), kind=kOutput, calls=%fused_computation.16 | convolution fusion | flops 3222011904 | bytes 9175040 | tf_op jit(solution)/shard_map/isbzc,sizra->rabc/dot_general | solution.py:90
  202.9 1.5 divide_bitcast_fusion.1
  204.4 3.9 %fusion.16 = bf16[16,2,16,16,128]{4,2,3,0,1:T(8,128)(2,1)S(1)} fusion(f32[1,256,16,128]{3,1,2,0:T(8,128)S(1)} %get-tuple-element.6, f32[1,256,16,128]{3,1,2,0:T(8,128)S(1)} %get-tuple-element.5, f32[1,256,1,16,16]{1,4,3,2,0:T(8,128)S(1)} %get-tuple-element.17, f32[1,256,1,16,16]{1,4,3,2,0:T(8,128)S(1)} %get-tuple-element.16, ...), kind=kOutput, calls=%fused_computation.19 | convolution fusion | flops 3224371200 | bytes 7077888 | tf_op jit(solution)/shard_map/sabc,sariz->irzbc/dot_general | solution.py:107
  208.3 1.9 copy.85
  210.2 12.7 %all-to-all-start.2 = ((bf16[16,2,16,16,128]{4,3,2,1,0:T(8,128)(2,1)}), bf16[16,2,16,16,128]{4,3,2,1,0:T(8,128)(2,1)S(1)}, u32[]{:S(2)}, u32[]{:S(2)}) async-start(bf16[16,2,16,16,128]{4,3,2,1,0:T(8,128)(2,1)} %copy.85), calls=%async_computation.2 | async-start | bytes 4194304 | tf_op jit(solution)/shard_map/all_to_all | solution.py:108
  222.9 3.1 %fusion.71 = (f32[1,16,16,1,4,64]{5,2,0,1,3,4:T(8,128)S(1)}, f32[1,16,16,1,4,64]{5,2,0,1,3,4:T(8,128)S(1)}, f32[1,16,16,1,4,64]{5,2,0,1,3,4:T(8,128)}) fusion(s32[4,64]{1,0:T(4,128)S(1)} %multiply_add_fusion.2, s32[16,16]{1,0:T(8,128)S(1)} %multiply_add_fusion), kind=kLoop, calls=%fused_computation.105 | loop fusion | flops 983040 | bytes 788480 | tf_op jit(solution)/shard_map/sin | solution.py:72
  226.0 26.2 %all-to-all-done.2 = bf16[16,2,16,16,128]{4,3,2,1,0:T(8,128)(2,1)S(1)} async-done(((bf16[16,2,16,16,128]{4,3,2,1,0:T(8,128)(2,1)}), bf16[16,2,16,16,128]{4,3,2,1,0:T(8,128)(2,1)S(1)}, u32[]{:S(2)}, u32[]{:S(2)}) %all-to-all-start.2) | async-done | bytes 2097184 | tf_op jit(solution)/shard_map/all_to_all | solution.py:108
  252.2 3.8 %convolution_bitcast_fusion = f32[4,2,16,64,128]{4,3,1,0,2:T(8,128)S(1)} fusion(f32[1,16,16,1,4,64]{5,2,0,1,3,4:T(8,128)} %get-tuple-element.14, f32[1,16,16,1,4,64]{5,2,0,1,3,4:T(8,128)S(1)} %get-tuple-element.13, f32[1,16,16,1,4,64]{5,2,0,1,3,4:T(8,128)S(1)} %get-tuple-element.12, bf16[16,2,16,16,128]{4,3,2,1,0:T(8,128)(2,1)S(1)} %all-to-all-done.2), kind=kOutput, calls=%fused_computation.17 | convolution fusion | flops 3222274048 | bytes 7077888 | tf_op jit(solution)/shard_map/iszbc,sibrjx->jrzxc/dot_general | solution.py:110
  255.9 0.6 copy.87
  256.5 51.5 %all_to_all.20 = f32[4,2,16,64,128]{4,3,1,2,0:T(8,128)S(1)} all-to-all(f32[4,2,16,64,128]{4,3,1,2,0:T(8,128)S(1)} %copy.87), channel_id=1, replica_groups=mesh['sta'=2,'gx'=16,'gy'=4] {'gy'}, dimensions={0} | all-to-all | bytes 8388608 | tf_op jit(solution)/shard_map/all_to_all | solution.py:111
  308.1 4.8 %fusion.33 = f32[1,16,64,512]{3,2,1,0:T(8,128)} fusion(f32[4,2,16,64,128]{4,3,1,2,0:T(8,128)S(1)} %all_to_all.20, f32[512,4,1,128]{3,0,2,1:T(8,128)S(1)} %copy-done.5, f32[512,4,1,128]{3,0,2,1:T(8,128)S(1)} %copy-done.3), kind=kOutput, calls=%fused_computation.45 | convolution fusion | flops 3222274048 | bytes 8388608 | tf_op jit(solution)/shard_map/jrzxc,yjrc->zxy/dot_general | solution.py:112
  (23 shorter events, 0.4 us)
Async XLA Ops:
  0.0 1.0 copy-start
  18.4 47.5 %collective-permute-start = (f32[16,64,512]{2,1,0:T(8,128)S(1)}, f32[16,64,512]{2,1,0:T(8,128)S(1)}, u32[]{:S(2)}, u32[]{:S(2)}) collective-permute-start(f32[16,64,512]{2,1,0:T(8,128)S(1)} %bitcast.134), channel_id=1, source_target_pairs={{0,64},{64,0},{1,65},{65,1},{2,66},{66,2},{3,67},{67,3},{4,68},{68... | collective-permute-start | bytes 6291464 | tf_op jit(solution)/shard_map/ppermute | solution.py:84
  24.4 41.5 %copy-start.2 = (f32[512,4,1,128]{3,0,2,1:T(8,128)}, f32[512,4,1,128]{3,0,2,1:T(8,128)S(1)}, u32[]{:S(2)}) copy-start(f32[512,4,1,128]{3,0,2,1:T(8,128)S(1)} %get-tuple-element.21) | copy-start | bytes 3145732
  24.4 41.5 %copy-start.4 = (f32[512,4,1,128]{3,0,2,1:T(8,128)}, f32[512,4,1,128]{3,0,2,1:T(8,128)S(1)}, u32[]{:S(2)}) copy-start(f32[512,4,1,128]{3,0,2,1:T(8,128)S(1)} %get-tuple-element.22) | copy-start | bytes 3145732
  71.7 53.3 %all-to-all-start = ((f32[4,2,16,64,128]{4,3,2,1,0:T(8,128)}), f32[4,2,16,64,128]{4,3,2,1,0:T(8,128)}, u32[]{:S(2)}, u32[]{:S(2)}) async-start(f32[4,2,16,64,128]{4,3,2,1,0:T(8,128)} %convolution_bitcast_fusion.1), calls=%async_computation | async-start | bytes 8388608 | tf_op jit(solution)/shard_map/all_to_all | solution.py:87
  133.8 63.5 %all-to-all-start.1 = ((f32[16,2,16,16,128]{4,3,1,2,0:T(8,128)}), f32[16,2,16,16,128]{4,3,1,2,0:T(8,128)}, u32[]{:S(2)}, u32[]{:S(2)}) async-start(f32[16,2,16,16,128]{4,3,1,2,0:T(8,128)} %copy.74), calls=%async_computation.1 | async-start | bytes 8388608 | tf_op jit(solution)/shard_map/all_to_all | solution.py:89
  197.3 5.6 %copy-start.6 = (f32[256,16,128]{2,1,0:T(8,128)S(1)}, f32[256,16,128]{2,1,0:T(8,128)}, u32[]{:S(2)}) copy-start(f32[256,16,128]{2,1,0:T(8,128)} %param.11) | copy-start | bytes 6291460
  197.3 5.6 %copy-start.7 = (f32[256,16,128]{2,1,0:T(8,128)S(1)}, f32[256,16,128]{2,1,0:T(8,128)}, u32[]{:S(2)}) copy-start(f32[256,16,128]{2,1,0:T(8,128)} %param.10) | copy-start | bytes 6291460
  210.2 42.0 %all-to-all-start.2 = ((bf16[16,2,16,16,128]{4,3,2,1,0:T(8,128)(2,1)}), bf16[16,2,16,16,128]{4,3,2,1,0:T(8,128)(2,1)S(1)}, u32[]{:S(2)}, u32[]{:S(2)}) async-start(bf16[16,2,16,16,128]{4,3,2,1,0:T(8,128)(2,1)} %copy.85), calls=%async_computation.2 | async-start | bytes 4194304 | tf_op jit(solution)/shard_map/all_to_all | solution.py:108
  256.5 51.5 %copy-start.3 = (f32[512,4,1,128]{3,0,2,1:T(8,128)S(1)}, f32[512,4,1,128]{3,0,2,1:T(8,128)}, u32[]{:S(2)}) copy-start(f32[512,4,1,128]{3,0,2,1:T(8,128)} %copy-done.2) | copy-start | bytes 3145732
  256.5 51.5 %copy-start.5 = (f32[512,4,1,128]{3,0,2,1:T(8,128)S(1)}, f32[512,4,1,128]{3,0,2,1:T(8,128)}, u32[]{:S(2)}) copy-start(f32[512,4,1,128]{3,0,2,1:T(8,128)} %copy-done.4) | copy-start | bytes 3145732
  308.1 4.8 %copy-start.1 = (f32[128,1024]{1,0:T(8,128)S(1)}, f32[128,1024]{1,0:T(8,128)}, u32[]{:S(2)}) copy-start(f32[128,1024]{1,0:T(8,128)} %param.6) | copy-start | bytes 1572868
